TPU v7x, 32 devices: a whole 2x2x4 slice. The times are simulated.
32 devices in a mesh: groups: 2 (over y), expert: 4 (over z), dp: 4 (over x, core).
Axes of the slice: x: 2, y: 2, z: 4, core: 2. Of those that a mesh axis runs over, the one named last changes fastest.
Arguments:
- out_grad: bfloat16 [4096, 2048], P(('groups', 'expert', 'dp')), parts along dimension 0, may hold values from -0.5 to 0.5
- gate_weights: bfloat16 [4096, 8], P(('groups', 'expert', 'dp')), parts along dimension 0, may hold values from 0.049804688 to 0.5
- expert_ids: int32 [4096, 8], P(('groups', 'expert', 'dp')), parts along dimension 0, may hold values from 0 to 31, all different within a row; in each aligned block of 128 rows (0 to 127, 128 to 255, ...) at most 36 rows name the same one
- hidden: bfloat16 [32, 8, 4, 36, 768], P('expert', ('groups', 'dp')), parts along dimension 1, may hold values from -6 to 6
- down_weight: bfloat16 [32, 768, 2048], P('expert', None, 'dp'), may hold values from -0.21875 to 0.21875
Outputs:
- weight_grad: float32 [64, 768, 2048], P(('groups', 'expert'), None, 'dp'), parts along dimension 0
- gate_grad: float32 [4096, 8], P(('groups', 'expert', 'dp')), parts along dimension 0
There are 2 independent parts, one for each index of `groups`. A program takes and returns all parts, laid end to end along the dimension named above; an argument that names none is the same for every part. Nothing has to cross between parts.
Inputs may be any that keep to these rules, and one draw needn't show every extreme that they name: `expert_ids`: each token names 8 different experts; within each block of 128 tokens (one device's tokens) no expert is named by more than 36 tokens, a bound that some block reaches.
All inputs are finite; a program needn't handle non-finite values.
Results may differ from a plain program's by a relative error of at most 0.0095.
Values may be sent and summed in bfloat16 or wider, within the bound.
No kernel may reach another device: no remote copies, remote signals or barrier semaphores. Data moves between devices by JAX's collectives and lax.ppermute only.
A program may use at most 128 MiB of HBM per device.

v0:
```python
import jax
import jax.numpy as jnp
from jax import lax
from jax.sharding import PartitionSpec as P


def per_device(out_grad, gate_weights, expert_ids, hidden, down_weight):
    tok_rows = out_grad.shape[0]
    top_count = expert_ids.shape[1]
    row_width = out_grad.shape[1]
    local_count = hidden.shape[0]
    peer_count = lax.axis_size("expert")
    expert_count = local_count * peer_count
    capacity = hidden.shape[3]
    hidden_width = hidden.shape[4]
    slot_rows = peer_count * capacity
    id_flat = expert_ids.reshape(-1)
    onehot = (id_flat[:, None] == jnp.arange(expert_count, dtype=jnp.int32)[None, :]).astype(
        jnp.int32
    )
    slot_index = jnp.sum((jnp.cumsum(onehot, axis=0) - 1) * onehot, axis=1)
    dest_index = id_flat * capacity + slot_index
    pair_count = tok_rows * top_count
    source_table = (
        jnp.full((expert_count * capacity,), pair_count, jnp.int32)
        .at[dest_index]
        .set(jnp.arange(pair_count, dtype=jnp.int32))
    )
    grad_ext = jnp.concatenate([out_grad, jnp.zeros((1, row_width), out_grad.dtype)], axis=0)
    gate_ext = jnp.concatenate(
        [gate_weights.reshape(-1), jnp.zeros((1,), gate_weights.dtype)], axis=0
    )
    send_grad = grad_ext[source_table // top_count].reshape(
        peer_count, local_count * capacity, row_width
    )
    send_gate = gate_ext[source_table].reshape(peer_count, local_count * capacity)
    recv_grad, recv_gate = (
        lax.all_to_all(send_grad, "expert", split_axis=0, concat_axis=0, tiled=True),
        lax.all_to_all(send_gate, "expert", split_axis=0, concat_axis=0, tiled=True),
    )
    recv_grad = recv_grad.reshape(peer_count, local_count, capacity, row_width).transpose(
        1, 0, 2, 3
    )
    recv_grad = recv_grad.reshape(local_count, slot_rows, row_width)
    recv_gate = recv_gate.reshape(peer_count, local_count, capacity).transpose(1, 0, 2)
    recv_gate = recv_gate.reshape(local_count, slot_rows)
    scaled = (recv_gate.astype(jnp.float32)[:, :, None] * recv_grad).astype(jnp.bfloat16)
    hidden_rows = hidden.reshape(local_count, slot_rows, hidden_width)
    shards = lax.axis_size("dp")
    column_part = scaled.reshape(local_count, slot_rows, shards, row_width // shards)
    columns_in = lax.all_to_all(column_part, "dp", split_axis=2, concat_axis=2, tiled=True)
    hidden_all = lax.all_gather(hidden_rows[:, None], "dp", axis=1, tiled=True)
    partial_value = jnp.einsum(
        "eirf,erid->eifd", hidden_all, columns_in, preferred_element_type=jnp.float32
    ).astype(jnp.bfloat16)
    weight_grad = jnp.sum(partial_value.astype(jnp.float32), axis=1)
    full_weight = lax.all_gather(down_weight, "dp", axis=2, tiled=True)
    expert_out = jnp.einsum(
        "erf,efd->erd", hidden_rows, full_weight, preferred_element_type=jnp.float32
    )
    slot_grad = jnp.sum(recv_grad * expert_out, axis=2)
    send_back = slot_grad.reshape(local_count, peer_count, capacity).transpose(1, 0, 2)
    send_back = send_back.reshape(peer_count, local_count * capacity)
    returned = lax.all_to_all(send_back, "expert", split_axis=0, concat_axis=0, tiled=True)
    gate_grad = returned.reshape(-1)[dest_index].reshape(tok_rows, top_count)
    return (weight_grad, gate_grad)


def solution(mesh):
    return jax.shard_map(
        per_device,
        mesh=mesh,
        in_specs=(
            P(("groups", "expert", "dp"), None),
            P(("groups", "expert", "dp"), None),
            P(("groups", "expert", "dp"), None),
            P("expert", ("groups", "dp"), None, None, None),
            P("expert", None, "dp"),
        ),
        out_specs=(P(("groups", "expert"), None, "dp"), P(("groups", "expert", "dp"), None)),
        check_vma=False,
    )
```

profile of v0, /device:TPU:0, one launch (start us, length us, event | category | flops | bytes accessed | tf_op | source)
XLA Modules:
  0.0 316.2 jit_solution(5351354100891161966)
XLA Ops:
  7.2 0.7 all-gather.5.cloned.1.call-update
  7.9 0.8 copy.44
  8.7 0.1 eq.29
  8.8 0.1 eq.25
  8.9 9.0 %reduce-window.6 = s32[32,8,128]{2,1,0:T(8,128)S(1)} reduce-window(s32[32,8,128]{2,1,0:T(8,128)S(1)} %fusion.5, s32[]{:T(128)} %constant.16.clone.1), window={size=1x1x128 pad=0_0x0_0x127_0}, to_apply=%region_0.0 | reduce-window | flops 4161536 | bytes 262148 | tf_op jit(solution)/shard_map/reduce-window
  17.9 0.1 slice.14
  18.0 0.1 copy.46
  18.2 0.1 copy.47
  18.3 0.1 copy.43
  18.4 0.1 mul.33
  18.5 0.1 copy.42
  18.6 0.1 reshape.103
  18.7 0.1 add_add_fusion
  18.9 4.3 %scatter_custom_fusion = s32[1152]{0:T(1024)S(1)} fusion(s32[1024]{0:T(1024)S(1)} %bitcast.43, s32[1024]{0:T(1024)S(1)} %iota.11, s32[]{:T(128)} %constant.12.clone.1), kind=kCustom, calls=%fused_computation.31 | custom fusion | bytes 4612 | tf_op jit(solution)/shard_map/scatter | solution.py:27
  23.3 7.3 %gather_fusion = bf16[1152]{0:T(1024)(128)(2,1)S(1)} fusion(bf16[1025]{0:T(1024)(128)(2,1)S(1)} %pad_maximum_fusion, s32[2048]{0:T(1024)S(1)} %get-tuple-element.11), kind=kCustom, calls=%fused_computation | custom fusion | bytes 9216 | tf_op jit(solution)/shard_map/gather | solution.py:36
  30.6 0.1 all_to_all.24
  30.7 0.5 broadcast.92
  31.2 0.7 reduce.4
  31.8 0.7 reshape.154
  32.5 6.3 %all-to-all-start = ((bf16[4,2,144]{2,1,0:T(2,128)(2,1)}), bf16[4,2,144]{2,1,0:T(2,128)(2,1)S(1)}, u32[]{:S(2)}, u32[]{:S(2)}) async-start(bf16[4,2,144]{2,1,0:T(2,128)(2,1)} %reshape.154), calls=%async_computation | async-start | bytes 8192 | tf_op jit(solution)/shard_map/all_to_all | solution.py:39
  38.9 5.9 %gather_fusion.1 = bf16[1152,2048]{1,0:T(8,128)(2,1)} fusion(bf16[129,2048]{1,0:T(8,128)(2,1)S(1)} %concatenate.7, s32[2048]{0:T(1024)S(1)} %get-tuple-element.10), kind=kCustom, calls=%fused_computation.1 | custom fusion | bytes 9441792 | tf_op jit(solution)/shard_map/gather | solution.py:33
  44.8 5.2 %all-to-all-start.1 = ((bf16[4,288,2048]{2,1,0:T(8,128)(2,1)}), bf16[4,288,2048]{2,1,0:T(8,128)(2,1)}, u32[]{:S(2)}, u32[]{:S(2)}) async-start(bf16[4,288,2048]{2,1,0:T(8,128)(2,1)} %bitcast.34), calls=%async_computation.1 | async-start | bytes 9437184 | tf_op jit(solution)/shard_map/all_to_all | solution.py:38
  50.0 0.2 all-gather.3.cloned.1.call-start
  50.2 0.5 copy.54
  50.8 1.2 copy-done
  52.0 1.6 copy.55
  53.5 0.1 reshape.155
  53.7 0.1 reshape.113
  53.8 0.1 reshape.110
  53.8 0.1 copy.50
  53.9 100.5 %all-to-all-done.1 = bf16[4,288,2048]{2,1,0:T(8,128)(2,1)} async-done(((bf16[4,288,2048]{2,1,0:T(8,128)(2,1)}), bf16[4,288,2048]{2,1,0:T(8,128)(2,1)}, u32[]{:S(2)}, u32[]{:S(2)}) %all-to-all-start.1) | async-done | bytes 4718624 | tf_op jit(solution)/shard_map/all_to_all | solution.py:38
  154.4 6.0 %copy.51 = f32[4,288,2048]{2,0,1:T(4,128)S(1)} copy(bf16[4,288,2048]{2,1,0:T(8,128)(2,1)} %all-to-all-done.1) | data formatting | bytes 14155776 | tf_op jit(solution)/shard_map/convert_element_type | solution.py:47
  160.4 9.2 %copy.52 = f32[8,4,36,2048]{3,0,2,1:T(8,128)} copy(f32[8,4,36,2048]{3,1,2,0:T(4,128)S(1)} %bitcast.33) | data formatting | bytes 18874368 | tf_op jit(solution)/shard_map/convert_element_type | solution.py:47
  169.6 12.6 %reshape.111 = f32[8,144,4,512]{3,2,0,1:T(4,128)} reshape(f32[8,4,36,2048]{3,0,2,1:T(8,128)} %copy.52) | data formatting | bytes 18874368 | tf_op jit(solution)/shard_map/convert_element_type | solution.py:47
  182.2 6.1 %multiply_convert_fusion = bf16[8,144,4,512]{3,2,0,1:T(4,128)(2,1)S(1)} fusion(f32[8,144,4,512]{3,2,0,1:T(4,128)} %reshape.111, f32[8,144]{0,1:T(8,128)S(1)} %copy.50), kind=kLoop, calls=%fused_computation.7 | loop fusion | flops 4718592 | bytes 14160384 | tf_op jit(solution)/shard_map/convert_element_type | solution.py:47
  188.2 4.8 %copy.53 = bf16[8,144,4,512]{3,1,0,2:T(8,128)(2,1)} copy(bf16[8,144,4,512]{3,2,0,1:T(4,128)(2,1)S(1)} %multiply_convert_fusion) | data formatting | bytes 9437184 | tf_op jit(solution)/shard_map/convert_element_type | solution.py:47
  193.0 5.2 %all-to-all-start.2 = ((bf16[8,144,4,512]{3,1,0,2:T(8,128)(2,1)}), bf16[8,144,4,512]{3,1,0,2:T(8,128)(2,1)}, u32[]{:S(2)}, u32[]{:S(2)}) async-start(bf16[8,144,4,512]{3,1,0,2:T(8,128)(2,1)} %copy.53), calls=%async_computation.2 | async-start | bytes 9437184 | tf_op jit(solution)/shard_map/all_to_all | solution.py:51
  198.3 20.2 %fusion = f32[8,144]{1,0:T(8,128)S(1)} fusion(f32[8,144,2048]{2,0,1:T(8,128)} %bitcast.32, bf16[8,768,2048]{2,1,0:T(8,128)(2,1)} %all-gather.5.cloned.1.call-done, bf16[8,144,768]{2,0,1:T(8,128)(2,1)S(1)} %bitcast.36), kind=kOutput, calls=%fused_computation.6 | convolution fusion | flops 3628596224 | bytes 36377088 | tf_op jit(solution)/shard_map/erf,efd->erd/dot_general | solution.py:58
  218.5 0.1 reshape.107
  218.6 0.7 all_to_all.25
  219.3 49.3 %all-to-all-done.2 = bf16[8,144,4,512]{3,1,0,2:T(8,128)(2,1)} async-done(((bf16[8,144,4,512]{3,1,0,2:T(8,128)(2,1)}), bf16[8,144,4,512]{3,1,0,2:T(8,128)(2,1)}, u32[]{:S(2)}, u32[]{:S(2)}) %all-to-all-start.2) | async-done | bytes 4718624 | tf_op jit(solution)/shard_map/all_to_all | solution.py:51
  268.6 4.6 %all-to-all-start.3 = ((f32[4,1,288]{2,1,0:T(1,128)}), f32[4,1,288]{2,1,0:T(1,128)S(1)}, u32[]{:S(2)}, u32[]{:S(2)}) async-start(f32[4,1,288]{2,1,0:T(1,128)} %all_to_all.25), calls=%async_computation.3 | async-start | bytes 12288 | tf_op jit(solution)/shard_map/all_to_all | solution.py:64
  273.2 16.6 %convert_reduce_fusion = f32[8,512,768]{2,1,0:T(8,128)} fusion(bf16[8,4,144,768]{3,2,1,0:T(8,128)(2,1)} %all-gather.3.cloned.1.call-done, bf16[8,144,4,512]{3,1,0,2:T(8,128)(2,1)} %all-to-all-done.2), kind=kOutput, calls=%fused_computation.4 | convolution fusion | flops 3658481664 | bytes 24379392 | tf_op jit(solution)/shard_map/eirf,erid->eifd/dot_general | solution.py:53
  289.7 12.6 %copy.63 = f32[8,768,512]{2,1,0:T(8,128)} copy(f32[8,768,512]{1,2,0:T(8,128)} %bitcast.37) | data formatting | bytes 25165824
  302.4 0.1 reshape.108
  302.4 6.2 %gather_fusion.2 = f32[1024]{0:T(1024)S(1)} fusion(f32[1152]{0:T(1024)S(1)} %reshape.108, s32[1024]{0:T(1024)S(1)} %broadcast_clamp_fusion), kind=kCustom, calls=%fused_computation.2 | custom fusion | bytes 12288 | tf_op jit(solution)/shard_map/gather | solution.py:65
  308.6 0.1 reshape.109
  308.7 0.7 copy.64
  (33 shorter events, 0.3 us)
Async XLA Ops:
  7.2 11.1 %copy-start.4 = (s32[128,8]{0,1:T(8,128)S(1)}, s32[128,8]{0,1:T(8,128)}, u32[]{:S(2)}) copy-start(s32[128,8]{0,1:T(8,128)} %param.7) | copy-start | bytes 12292
  7.2 11.3 %copy-start.5 = (bf16[128,8]{0,1:T(8,128)(2,1)S(1)}, bf16[128,8]{0,1:T(8,128)(2,1)}, u32[]{:S(2)}) copy-start(bf16[128,8]{0,1:T(8,128)(2,1)} %param.6) | copy-start | bytes 6148
  7.2 31.7 %copy-start.3 = (bf16[128,2048]{1,0:T(8,128)(2,1)S(1)}, bf16[128,2048]{1,0:T(8,128)(2,1)}, u32[]{:S(2)}) copy-start(bf16[128,2048]{1,0:T(8,128)(2,1)} %param.5) | copy-start | bytes 1572868
  7.2 191.1 %all-gather.5.cloned.1.call-start = ((), (), s32[]{:S(2)}) async-start(), calls=%async_computation.5 | async-start | bytes 31457280 | tf_op jit(solution)/shard_map/all_gather | solution.py:57
  32.5 12.3 %all-to-all-start = ((bf16[4,2,144]{2,1,0:T(2,128)(2,1)}), bf16[4,2,144]{2,1,0:T(2,128)(2,1)S(1)}, u32[]{:S(2)}, u32[]{:S(2)}) async-start(bf16[4,2,144]{2,1,0:T(2,128)(2,1)} %reshape.154), calls=%async_computation | async-start | bytes 8192 | tf_op jit(solution)/shard_map/all_to_all | solution.py:39
  44.8 5.4 %copy-start.2 = (bf16[8,1,4,36,768]{4,2,3,1,0:T(4,128)(2,1)S(1)}, bf16[8,1,4,36,768]{4,2,3,1,0:T(4,128)(2,1)}, u32[]{:S(2)}) copy-start(bf16[8,1,4,36,768]{4,2,3,1,0:T(4,128)(2,1)} %param.8) | copy-start | bytes 5308420
  44.8 109.6 %all-to-all-start.1 = ((bf16[4,288,2048]{2,1,0:T(8,128)(2,1)}), bf16[4,288,2048]{2,1,0:T(8,128)(2,1)}, u32[]{:S(2)}, u32[]{:S(2)}) async-start(bf16[4,288,2048]{2,1,0:T(8,128)(2,1)} %bitcast.34), calls=%async_computation.1 | async-start | bytes 9437184 | tf_op jit(solution)/shard_map/all_to_all | solution.py:38
  50.0 223.1 %all-gather.3.cloned.1.call-start = ((), (), s32[]{:S(2)}) async-start(), calls=%async_computation.4 | async-start | bytes 8847360 | tf_op jit(solution)/shard_map/all_gather | solution.py:52
  50.8 1.2 copy-start
  193.0 5.2 %copy-start.1 = (bf16[8,1,4,36,768]{4,0,3,2,1:T(8,128)(2,1)S(1)}, bf16[8,1,4,36,768]{4,0,3,2,1:T(8,128)(2,1)}, u32[]{:S(2)}) copy-start(bf16[8,1,4,36,768]{4,0,3,2,1:T(8,128)(2,1)} %copy-done) | copy-start | bytes 5308420
  193.0 75.5 %all-to-all-start.2 = ((bf16[8,144,4,512]{3,1,0,2:T(8,128)(2,1)}), bf16[8,144,4,512]{3,1,0,2:T(8,128)(2,1)}, u32[]{:S(2)}, u32[]{:S(2)}) async-start(bf16[8,144,4,512]{3,1,0,2:T(8,128)(2,1)} %copy.53), calls=%async_computation.2 | async-start | bytes 9437184 | tf_op jit(solution)/shard_map/all_to_all | solution.py:51
  268.6 33.8 %all-to-all-start.3 = ((f32[4,1,288]{2,1,0:T(1,128)}), f32[4,1,288]{2,1,0:T(1,128)S(1)}, u32[]{:S(2)}, u32[]{:S(2)}) async-start(f32[4,1,288]{2,1,0:T(1,128)} %all_to_all.25), calls=%async_computation.3 | async-start | bytes 12288 | tf_op jit(solution)/shard_map/all_to_all | solution.py:64
Sparse Core Ops, SparseCore 0:
  9.6 157.5 all-gather.4
  168.7 67.3 all-gather.2
where the time goes:
time: 317 us; the launch traced here: 316 us
  waiting for transfers between devices  150 us (47%)
  local copies, waits for them, and re-layouts  77.1 us (24%)
  matrix products  36.8 us (12%)
  starting transfers between devices  21.5 us (7%)
  other arithmetic  16 us (5%)
  between operations  14.3 us (5%)
    all_to_all x1, waiting for transfers between devices, per_device(): lax.all_to_all(send_grad, 'expert', split_axis=0, concat_axis=0, tiled=True)  100 us
    all_to_all x1, waiting for transfers between devices, per_device(): lax.all_to_all(column_part, 'dp', split_axis=2, concat_axis=2, tiled=True)  49.3 us
    convert_element_type x7, local copies, waits for them, and re-layouts, per_device(): recv_gate.astype(jnp.float32)[:, :, None] * recv_grad  28 us
    dot_general x1, matrix products, per_device(): jnp.einsum('erf,efd->erd', hidden_rows, full_weight, preferred_element_ty...  20.2 us
    unnamed x19, local copies, waits for them, and re-layouts  16.7 us
    dot_general x1, matrix products, per_device(): jnp.einsum('eirf,erid->eifd', hidden_all, columns_in, preferred_element_t...  16.6 us
    another operation x2, other arithmetic  9.04 us
    gather x1, local copies, waits for them, and re-layouts, per_device(): gate_ext[source_table].reshape(peer_count, local_count * capacity)  7.27 us
  transfers between devices with their start and end apart: 6, of which 2 were waited for; matrix products, arithmetic and copies ran while one was open for 38% of the time, Pallas kernels for 0%

commit v1 on v0

v1 whole, which is shorter than its diff:
```python
import jax
import jax.numpy as jnp
from jax import lax
from jax.sharding import PartitionSpec as P


def per_device(out_grad, gate_weights, expert_ids, hidden, down_weight):
    tok_rows, top_count = expert_ids.shape
    row_width = out_grad.shape[1]
    local_count = hidden.shape[0]
    source_count = hidden.shape[2]
    capacity = hidden.shape[3]
    hidden_width = hidden.shape[4]
    peer_count = lax.axis_size("expert")
    shards = lax.axis_size("dp")
    expert_count = local_count * peer_count
    col_width = row_width // shards
    block_count = peer_count * shards
    f32 = jnp.float32
    bf16 = jnp.bfloat16

    cols = out_grad.reshape(tok_rows, shards, col_width)
    cols = lax.all_to_all(cols, "dp", split_axis=1, concat_axis=0, tiled=True)
    cols = cols.reshape(shards, tok_rows, col_width)
    grad_all = lax.all_gather(cols, "expert", axis=0, tiled=False)
    grad_all = grad_all.reshape(block_count, tok_rows, col_width)

    ids_all = lax.all_gather(expert_ids, ("expert", "dp"), axis=0, tiled=True)
    ids_all = ids_all.reshape(block_count, tok_rows, top_count)
    gate_all = lax.all_gather(gate_weights, ("expert", "dp"), axis=0, tiled=True)
    gate_all = gate_all.reshape(block_count, tok_rows, top_count)

    hidden_all = lax.all_gather(hidden, "dp", axis=1, tiled=True)

    my_experts = lax.axis_index("expert") * local_count + jnp.arange(local_count, dtype=jnp.int32)
    hit = ids_all[:, :, :, None] == my_experts[None, None, None, :]
    chose = jnp.any(hit, axis=2)
    gate_hit = jnp.sum(jnp.where(hit, gate_all.astype(f32)[:, :, :, None], 0.0), axis=2)
    before = (jnp.arange(tok_rows)[:, None] < jnp.arange(tok_rows)[None, :]).astype(bf16)
    rank = jnp.einsum(
        "bul,ut->btl", chose.astype(bf16), before, preferred_element_type=f32
    ).astype(jnp.int32)
    slot_ids = jnp.arange(capacity, dtype=jnp.int32)
    chose_t = chose.transpose(0, 2, 1)
    rank_t = rank.transpose(0, 2, 1)
    gate_t = gate_hit.transpose(0, 2, 1)
    select = chose_t[:, :, None, :] & (rank_t[:, :, None, :] == slot_ids[None, None, :, None])
    select_gate = jnp.where(select, gate_t[:, :, None, :], 0.0).astype(bf16)
    grad_rows = jnp.einsum(
        "blct,btd->blcd", select.astype(bf16), grad_all, preferred_element_type=f32
    ).astype(bf16)
    scaled = jnp.einsum(
        "blct,btd->blcd", select_gate, grad_all, preferred_element_type=f32
    ).astype(bf16)
    grad_rows = grad_rows.reshape(peer_count, shards, local_count, capacity, col_width)
    scaled = scaled.reshape(peer_count, shards, local_count, capacity, col_width)

    weight_grad = None
    for replica in range(shards):
        part = jnp.einsum(
            "lscf,slcd->lfd",
            hidden_all[:, replica],
            scaled[:, replica],
            preferred_element_type=f32,
        ).astype(bf16).astype(f32)
        weight_grad = part if weight_grad is None else weight_grad + part

    expert_out = jnp.einsum(
        "liscf,lfd->silcd", hidden_all, down_weight, preferred_element_type=f32
    )
    slot_part = jnp.sum(grad_rows.astype(f32) * expert_out, axis=4)
    send_back = slot_part.reshape(block_count, local_count, capacity)
    returned = lax.all_to_all(
        send_back, ("expert", "dp"), split_axis=0, concat_axis=0, tiled=True
    )
    returned = returned.reshape(peer_count, shards, local_count, capacity)
    slot_grad = jnp.sum(returned, axis=1).reshape(expert_count * capacity)

    own_chose = jnp.any(
        expert_ids[:, :, None] == jnp.arange(expert_count, dtype=jnp.int32)[None, None, :], axis=1
    )
    own_rank = jnp.einsum(
        "ue,ut->te", own_chose.astype(bf16), before, preferred_element_type=f32
    ).astype(jnp.int32)
    own_slot = jnp.take_along_axis(own_rank, expert_ids, axis=1)
    gate_grad = slot_grad[expert_ids * capacity + own_slot]
    return (weight_grad, gate_grad)


def solution(mesh):
    return jax.shard_map(
        per_device,
        mesh=mesh,
        in_specs=(
            P(("groups", "expert", "dp"), None),
            P(("groups", "expert", "dp"), None),
            P(("groups", "expert", "dp"), None),
            P("expert", ("groups", "dp"), None, None, None),
            P("expert", None, "dp"),
        ),
        out_specs=(P(("groups", "expert"), None, "dp"), P(("groups", "expert", "dp"), None)),
        check_vma=False,
    )
```

time: 317 us -> 190 us (0.60)
  waiting for transfers between devices: 150 us -> 37.1 us
  blocking collectives: 0 us -> 52.1 us
  local copies, waits for them, and re-layouts: 77.1 us -> 38.8 us
  starting transfers between devices: 21.5 us -> 4.8 us
  other arithmetic: 16 us -> 1.04 us
  matrix products: 36.8 us -> 41.3 us
    all_to_all x4 -> x1, waiting for transfers between devices: 150 us -> 0.01 us  [per_device(): lax.all_to_all(send_back, ('expert', 'dp'), split_axis=0, concat_axis=0,...]
    all_gather x0 -> x2, blocking collectives: none -> 39.3 us  [the longest x1 21.2 us: per_device(): lax.all_gather(gate_weights, ('expert', 'dp'), axis=0, tiled=True)]
    all_gather x2, waiting for transfers between devices: 0.02 us -> 37 us  [the longest x1 37 us: per_device(): hidden_all = lax.all_gather(hidden, 'dp', axis=1, tiled=True)]
    convert_element_type x8 -> x0, local copies, waits for them, and re-layouts: 32.8 us -> none  [the longest x7 28 us: per_device(): recv_gate.astype(jnp.float32)[:, :, None] * recv_grad]
    all_to_all x4 -> x1, starting transfers between devices: 21.3 us -> 4.72 us  [per_device(): lax.all_to_all(send_back, ('expert', 'dp'), split_axis=0, concat_axis=0,...]
    all_to_all x0 -> x1, blocking collectives: none -> 12.9 us  [per_device(): cols = lax.all_to_all(cols, 'dp', split_axis=1, concat_axis=0, tiled=True)]
    another operation x2 -> x0, other arithmetic: 9.04 us -> none
    convert_element_type x3 -> x1, other arithmetic: 6.11 us -> 0.01 us  [per_device(): gate_all.astype(f32)[:, :, :, None]]
  transfers between devices with their start and end apart: 6 -> 3, of which waited for: 2 -> 1; matrix products, arithmetic and copies ran while one was open for 38% -> 31% of each run, Pallas kernels for 0% -> 0%
where the time goes in v1:
time: 190 us; the launch traced here: 189 us
  blocking collectives  52.1 us (27%)
  matrix products  41.3 us (22%)
  local copies, waits for them, and re-layouts  38.8 us (20%)
  waiting for transfers between devices  37.1 us (20%)
  between operations  14.3 us (8%)
  starting transfers between devices  4.8 us (3%)
    all_gather x1, waiting for transfers between devices, per_device(): hidden_all = lax.all_gather(hidden, 'dp', axis=1, tiled=True)  37 us
    all_gather x1, blocking collectives, per_device(): lax.all_gather(gate_weights, ('expert', 'dp'), axis=0, tiled=True)  21.2 us
    dot_general x4, matrix products, per_device(): jnp.einsum('lscf,slcd->lfd', hidden_all[:, replica], scaled[:, replica],...  20.7 us
    all_gather x1, blocking collectives, per_device(): ids_all = lax.all_gather(expert_ids, ('expert', 'dp'), axis=0, tiled=True)  18.1 us
    unnamed x18, local copies, waits for them, and re-layouts  17.8 us
    all_to_all x1, blocking collectives, per_device(): cols = lax.all_to_all(cols, 'dp', split_axis=1, concat_axis=0, tiled=True)  12.9 us
    dot_general x1, matrix products, per_device(): jnp.einsum('liscf,lfd->silcd', hidden_all, down_weight, preferred_element...  11.1 us
    gather x5, local copies, waits for them, and re-layouts, per_device(): own_slot = jnp.take_along_axis(own_rank, expert_ids, axis=1)  7.34 us
  transfers between devices with their start and end apart: 3, of which 1 were waited for; matrix products, arithmetic and copies ran while one was open for 31% of the time, Pallas kernels for 0%

profile of v1, /device:TPU:0, one launch (start us, length us, event | category | flops | bytes accessed | tf_op | source)
XLA Modules:
  0.0 189.4 jit_solution(14676324695385926704)
XLA Ops:
  7.2 0.0 copy-start.1
  7.2 0.0 all-gather.6.cloned.1.call-start
  7.2 1.4 copy.113
  8.7 12.9 %all_to_all.20 = bf16[128,4,512]{0,2,1:T(8,128)(2,1)S(1)} all-to-all(bf16[128,4,512]{0,2,1:T(8,128)(2,1)S(1)} %bitcast.95), channel_id=1, replica_groups=mesh['groups'=2,'expert'=4,'dp'=4] {'dp'}, dimensions={1} | all-to-all | bytes 1048576 | tf_op jit(solution)/shard_map/all_to_all | solution.py:23
  21.5 1.0 copy.114
  22.5 0.0 all-gather.6.cloned.1.call-update
  22.6 0.0 copy-start.4
  22.6 0.0 all-gather.4.cloned.1.call-start
  22.6 0.0 copy-done.1
  22.6 1.8 copy.116
  24.4 0.0 all-gather.4.cloned.1.call-update
  24.4 0.0 copy-done.4
  24.5 0.1 copy.127
  24.6 0.1 reshape.69
  24.7 0.1 convolution_convert_fusion.3
  24.8 7.0 %gather_fusion.1 = s32[1024]{0:T(1024)S(1)} fusion(s32[128,32]{0,1:T(8,128)S(1)} %convolution_convert_fusion.3, s32[1024]{0:T(1024)S(1)} %reshape.69), kind=kCustom, calls=%fused_computation.1 | custom fusion | bytes 16384 | tf_op jit(solution)/shard_map/jit(take_along_axis)/gather | solution.py:85
  31.9 0.1 reshape.72
  32.0 0.1 copy.129
  32.1 0.1 reshape.63
  32.2 0.0 copy-done.5
  32.2 21.2 %all_gather.13 = bf16[2048,8]{0,1:T(8,128)(2,1)S(1)} all-gather(bf16[128,8]{0,1:T(8,128)(2,1)S(1)} %copy-done.5), channel_id=1, replica_groups=mesh['groups'=2,'expert'=4,'dp'=4] {'expert','dp'}, dimensions={0}, use_global_device_ids=true | all-gather | bytes 34816 | tf_op jit(solution)/shard_map/all_gather | solution.py:30
  53.4 18.1 %all_gather.12 = s32[2048,8]{0,1:T(8,128)S(1)} all-gather(s32[128,8]{0,1:T(8,128)S(1)} %copy-done.4), channel_id=1, replica_groups=mesh['groups'=2,'expert'=4,'dp'=4] {'expert','dp'}, dimensions={0}, use_global_device_ids=true | all-gather | bytes 69632 | tf_op jit(solution)/shard_map/all_gather | solution.py:28
  71.5 0.1 compare_reduce_fusion
  71.7 0.1 fusion.21
  71.8 0.1 convolution_convert_fusion.2
  72.0 0.0 all-gather.6.cloned.1.call-done
  72.0 3.1 %convolution_convert_fusion = bf16[16,8,36,512]{3,2,1,0:T(8,128)(2,1)S(1)} fusion(bf16[16,128,1,512]{3,1,2,0:T(8,128)(2,1)} %all-gather.6.cloned.1.call-done, bf16[16,8,128]{2,1,0:T(8,128)(2,1)S(1)} %bitcast.101, s32[16,8,128]{2,1,0:T(8,128)S(1)} %convolution_convert_fusion.2, pred[16,8,128]{2,1,0:T(8,128)(4,1)S(1)} %bitcast.98), kind=kOutput, calls=%fused_computation.12 | convolution fusion | flops 608108544 | bytes 6930432 | tf_op jit(solution)/shard_map/blct,btd->blcd/dot_general | solution.py:52
  75.1 2.0 %fusion.27 = (bf16[4,1,8,36,512]{4,3,2,1,0:T(8,128)(2,1)S(1)}, bf16[4,1,8,36,512]{4,3,2,1,0:T(8,128)(2,1)}, bf16[4,1,8,36,512]{4,3,2,1,0:T(8,128)(2,1)}, bf16[4,1,8,36,512]{4,3,2,1,0:T(8,128)(2,1)S(1)}) fusion(bf16[4,4,8,36,512]{4,3,2,1,0:T(8,128)(2,1)S(1)} %bitcast.93), kind=kLoop, calls=%fused_computation.55 | loop fusion | bytes 9437184 | tf_op jit(solution)/shard_map/slice | solution.py:63
  77.1 0.5 copy-done
  77.6 6.0 %bitcast_convert_fusion.5 = f32[4,4,8,36,512]{4,3,2,1,0:T(8,128)} fusion(bf16[16,128,1,512]{3,1,2,0:T(8,128)(2,1)S(1)} %copy-done, s32[16,8,128]{2,1,0:T(8,128)S(1)} %convolution_convert_fusion.2, pred[16,8,128]{2,1,0:T(8,128)(4,1)S(1)} %bitcast.99), kind=kOutput, calls=%fused_computation.52 | convolution fusion | flops 609878016 | bytes 11616256 | tf_op jit(solution)/shard_map/blct,btd->blcd/dot_general | solution.py:49
  83.7 37.0 %all-gather.4.cloned.1.call-done = bf16[8,4,4,36,768]{4,0,3,2,1:T(8,128)(2,1)} async-done(((bf16[8,1,4,36,768]{4,0,3,2,1:T(8,128)(2,1)}), bf16[8,4,4,36,768]{4,0,3,2,1:T(8,128)(2,1)}) %all-gather.4.cloned.1.call-update) | async-done | bytes 7077904 | tf_op jit(solution)/shard_map/all_gather | solution.py:33
  120.7 11.1 %fusion = f32[4,4,8,36]{3,0,1,2:T(4,128)S(1)} fusion(f32[4,4,8,36,512]{4,3,2,1,0:T(8,128)} %bitcast_convert_fusion.5, bf16[8,4,4,36,768]{4,0,3,2,1:T(8,128)(2,1)} %all-gather.4.cloned.1.call-done, bf16[8,768,512]{2,1,0:T(8,128)(2,1)} %param.9), kind=kOutput, calls=%fused_computation.8 | convolution fusion | flops 3628592640 | bytes 22824960 | tf_op jit(solution)/shard_map/liscf,lfd->silcd/dot_general | solution.py:68
  131.8 0.7 reshape.91
  132.5 4.7 %all-to-all-start.1 = ((f32[16,1,288]{2,1,0:T(1,128)}), f32[16,1,288]{2,1,0:T(1,128)S(1)}, u32[]{:S(2)}, u32[]{:S(2)}) async-start(f32[16,1,288]{2,1,0:T(1,128)} %reshape.91), calls=%async_computation.1 | async-start | bytes 49152 | tf_op jit(solution)/shard_map/all_to_all | solution.py:73
  137.3 3.6 %fusion.26 = (bf16[8,1,4,36,768]{4,0,3,2,1:T(8,128)(2,1)S(1)}, bf16[8,1,4,36,768]{4,0,3,2,1:T(8,128)(2,1)S(1)}, bf16[8,1,4,36,768]{4,0,3,2,1:T(8,128)(2,1)S(1)}, bf16[8,1,4,36,768]{4,0,3,2,1:T(8,128)(2,1)S(1)}) fusion(bf16[8,4,4,36,768]{4,0,3,2,1:T(8,128)(2,1)} %all-gather.4.cloned.1.call-done), kind=kLoop, calls=%fused_computation.54 | loop fusion | bytes 14155776 | tf_op jit(solution)/shard_map/slice | solution.py:62
  140.9 2.0 %fusion.12 = bf16[8,512,768,1]{2,1,3,0:T(8,128)(2,1)S(1)} fusion(bf16[8,1,4,36,768]{4,0,3,2,1:T(8,128)(2,1)S(1)} %get-tuple-element.15, bf16[4,1,8,36,512]{4,3,2,1,0:T(8,128)(2,1)S(1)} %copy-done.3), kind=kOutput, calls=%fused_computation.21 | convolution fusion | flops 905969664 | bytes 9240576 | tf_op jit(solution)/shard_map/lscf,slcd->lfd/dot_general | solution.py:60
  143.0 4.7 %fusion.13 = bf16[8,512,768,1]{2,1,3,0:T(8,128)(2,1)} fusion(bf16[8,1,4,36,768]{4,0,3,2,1:T(8,128)(2,1)S(1)} %get-tuple-element.16, bf16[4,1,8,36,512]{4,3,2,1,0:T(8,128)(2,1)S(1)} %copy-done.2), kind=kOutput, calls=%fused_computation.23 | convolution fusion | flops 905969664 | bytes 9240576 | tf_op jit(solution)/shard_map/lscf,slcd->lfd/dot_general | solution.py:60
  147.6 4.8 %fusion.14 = bf16[8,512,768,1]{2,1,3,0:T(8,128)(2,1)} fusion(bf16[8,1,4,36,768]{4,0,3,2,1:T(8,128)(2,1)S(1)} %get-tuple-element.17, bf16[4,1,8,36,512]{4,3,2,1,0:T(8,128)(2,1)S(1)} %get-tuple-element.21), kind=kOutput, calls=%fused_computation.25 | convolution fusion | flops 905969664 | bytes 9240576 | tf_op jit(solution)/shard_map/lscf,slcd->lfd/dot_general | solution.py:60
  152.4 9.2 %add_bitcast_fusion = f32[8,768,512]{1,2,0:T(8,128)} fusion(bf16[8,512,768,1]{2,1,3,0:T(8,128)(2,1)} %fusion.14, bf16[8,512,768,1]{2,1,3,0:T(8,128)(2,1)} %fusion.13, bf16[8,512,768,1]{2,1,3,0:T(8,128)(2,1)S(1)} %fusion.12, bf16[8,1,4,36,768]{4,0,3,2,1:T(8,128)(2,1)S(1)} %get-tuple-element.14, bf16[4,1,8,36,512]{4,3,2,1,0:T(8,128)(2,1)S(1)} %get-tuple-element.18), kind=kOutput, calls=%fused_computation.6 | convolution fusion | flops 931135488 | bytes 34406400 | tf_op jit(solution)/shard_map/lscf,slcd->lfd/dot_general | solution.py:60
  161.6 12.6 %copy.130 = f32[8,768,512]{2,1,0:T(8,128)} copy(f32[8,768,512]{1,2,0:T(8,128)} %add_bitcast_fusion) | data formatting | bytes 25165824
  174.2 0.0 all-to-all-done.1
  174.2 0.5 broadcast.36
  174.7 0.7 reduce
  175.5 0.1 reshape.92
  175.6 0.1 reshape.57
  175.7 6.2 %gather_fusion = f32[1024]{0:T(1024)S(1)} fusion(f32[1152]{0:T(1024)S(1)} %reshape.57, s32[1024]{0:T(1024)S(1)} %broadcast_clamp_fusion), kind=kCustom, calls=%fused_computation | custom fusion | bytes 12288 | tf_op jit(solution)/shard_map/gather | solution.py:86
  181.8 0.1 reshape.62
  181.9 0.7 copy.131
  (15 shorter events, 0.1 us)
Async XLA Ops:
  7.2 15.5 %copy-start.1 = (bf16[8,1,4,36,768]{4,2,3,1,0:T(4,128)(2,1)S(1)}, bf16[8,1,4,36,768]{4,2,3,1,0:T(4,128)(2,1)}, u32[]{:S(2)}) copy-start(bf16[8,1,4,36,768]{4,2,3,1,0:T(4,128)(2,1)} %param.8) | copy-start | bytes 5308420
  7.2 64.8 %all-gather.6.cloned.1.call-start = ((), (), s32[]{:S(2)}) async-start(), calls=%async_computation.3 | async-start | bytes 2621440 | tf_op jit(solution)/shard_map/all_gather | solution.py:25
  22.6 1.9 copy-start.4
  22.6 98.1 %all-gather.4.cloned.1.call-start = ((), (), s32[]{:S(2)}) async-start(), calls=%async_computation.2 | async-start | bytes 8847360 | tf_op jit(solution)/shard_map/all_gather | solution.py:33
  24.8 7.4 %copy-start.5 = (bf16[128,8]{0,1:T(8,128)(2,1)S(1)}, bf16[128,8]{0,1:T(8,128)(2,1)}, u32[]{:S(2)}) copy-start(bf16[128,8]{0,1:T(8,128)(2,1)} %param.6) | copy-start | bytes 6148
  75.1 2.5 %copy-start = (bf16[16,128,1,512]{3,1,2,0:T(8,128)(2,1)S(1)}, bf16[16,128,1,512]{3,1,2,0:T(8,128)(2,1)}, u32[]{:S(2)}) copy-start(bf16[16,128,1,512]{3,1,2,0:T(8,128)(2,1)} %all-gather.6.cloned.1.call-done) | copy-start | bytes 6291460
  132.5 41.7 %all-to-all-start.1 = ((f32[16,1,288]{2,1,0:T(1,128)}), f32[16,1,288]{2,1,0:T(1,128)S(1)}, u32[]{:S(2)}, u32[]{:S(2)}) async-start(f32[16,1,288]{2,1,0:T(1,128)} %reshape.91), calls=%async_computation.1 | async-start | bytes 49152 | tf_op jit(solution)/shard_map/all_to_all | solution.py:73
  137.3 3.6 %copy-start.3 = (bf16[4,1,8,36,512]{4,3,2,1,0:T(8,128)(2,1)S(1)}, bf16[4,1,8,36,512]{4,3,2,1,0:T(8,128)(2,1)}, u32[]{:S(2)}) copy-start(bf16[4,1,8,36,512]{4,3,2,1,0:T(8,128)(2,1)} %get-tuple-element.19) | copy-start | bytes 3538948
  140.9 2.1 %copy-start.2 = (bf16[4,1,8,36,512]{4,3,2,1,0:T(8,128)(2,1)S(1)}, bf16[4,1,8,36,512]{4,3,2,1,0:T(8,128)(2,1)}, u32[]{:S(2)}) copy-start(bf16[4,1,8,36,512]{4,3,2,1,0:T(8,128)(2,1)} %get-tuple-element.20) | copy-start | bytes 3538948
Sparse Core Ops, SparseCore 0:
  22.7 46.6 all-gather.5
  70.9 49.7 all-gather.3

commit v2 on v1

--- a/solution.py
+++ b/solution.py
@@ -8,9 +8,7 @@
     tok_rows, top_count = expert_ids.shape
     row_width = out_grad.shape[1]
     local_count = hidden.shape[0]
-    source_count = hidden.shape[2]
     capacity = hidden.shape[3]
-    hidden_width = hidden.shape[4]
     peer_count = lax.axis_size("expert")
     shards = lax.axis_size("dp")
     expert_count = local_count * peer_count
@@ -18,19 +16,30 @@
     block_count = peer_count * shards
     f32 = jnp.float32
     bf16 = jnp.bfloat16
+    my_dp = lax.axis_index("dp")
 
+    fetched = lax.ppermute(hidden, "dp", [(j, j ^ 2) for j in range(shards)])
+    paired = lax.ppermute(
+        jnp.concatenate([hidden, fetched], axis=1), "dp", [(j, j ^ 1) for j in range(shards)]
+    )
+    pieces = [hidden, fetched, paired[:, 0:1], paired[:, 1:2]]
+    piece_replica = [my_dp, my_dp ^ 2, my_dp ^ 1, my_dp ^ 3]
+
+    meta = jnp.concatenate([expert_ids.astype(bf16), gate_weights], axis=1).reshape(-1)
+    meta_len = meta.shape[0]
+    meta_rows = -(-meta_len // col_width)
+    meta = jnp.pad(meta, (0, meta_rows * col_width - meta_len)).reshape(meta_rows, 1, col_width)
     cols = out_grad.reshape(tok_rows, shards, col_width)
+    cols = jnp.concatenate([cols, jnp.broadcast_to(meta, (meta_rows, shards, col_width))], axis=0)
     cols = lax.all_to_all(cols, "dp", split_axis=1, concat_axis=0, tiled=True)
-    cols = cols.reshape(shards, tok_rows, col_width)
-    grad_all = lax.all_gather(cols, "expert", axis=0, tiled=False)
-    grad_all = grad_all.reshape(block_count, tok_rows, col_width)
-
-    ids_all = lax.all_gather(expert_ids, ("expert", "dp"), axis=0, tiled=True)
-    ids_all = ids_all.reshape(block_count, tok_rows, top_count)
-    gate_all = lax.all_gather(gate_weights, ("expert", "dp"), axis=0, tiled=True)
-    gate_all = gate_all.reshape(block_count, tok_rows, top_count)
-
-    hidden_all = lax.all_gather(hidden, "dp", axis=1, tiled=True)
+    cols = cols.reshape(shards, tok_rows + meta_rows, col_width)
+    got = lax.all_gather(cols, "expert", axis=0, tiled=False)
+    got = got.reshape(block_count, tok_rows + meta_rows, col_width)
+    grad_all = got[:, :tok_rows]
+    meta_all = got[:, tok_rows:].reshape(block_count, meta_rows * col_width)[:, :meta_len]
+    meta_all = meta_all.reshape(block_count, tok_rows, 2 * top_count)
+    ids_all = meta_all[:, :, :top_count].astype(jnp.int32)
+    gate_all = meta_all[:, :, top_count:]
 
     my_experts = lax.axis_index("expert") * local_count + jnp.arange(local_count, dtype=jnp.int32)
     hit = ids_all[:, :, :, None] == my_experts[None, None, None, :]
@@ -56,34 +65,38 @@
     scaled = scaled.reshape(peer_count, shards, local_count, capacity, col_width)
 
     weight_grad = None
-    for replica in range(shards):
+    slot_part = jnp.zeros((peer_count, shards, local_count, capacity), f32)
+    for piece, replica in zip(pieces, piece_replica):
+        piece = piece[:, 0]
+        scaled_r = lax.dynamic_index_in_dim(scaled, replica, axis=1, keepdims=False)
+        rows_r = lax.dynamic_index_in_dim(grad_rows, replica, axis=1, keepdims=False)
         part = jnp.einsum(
-            "lscf,slcd->lfd",
-            hidden_all[:, replica],
-            scaled[:, replica],
-            preferred_element_type=f32,
+            "lscf,slcd->lfd", piece, scaled_r, preferred_element_type=f32
         ).astype(bf16).astype(f32)
         weight_grad = part if weight_grad is None else weight_grad + part
+        expert_out = jnp.einsum(
+            "lscf,lfd->slcd", piece, down_weight, preferred_element_type=f32
+        )
+        slot_r = jnp.sum(rows_r.astype(f32) * expert_out, axis=3)
+        slot_part = lax.dynamic_update_index_in_dim(slot_part, slot_r, replica, axis=1)
 
-    expert_out = jnp.einsum(
-        "liscf,lfd->silcd", hidden_all, down_weight, preferred_element_type=f32
-    )
-    slot_part = jnp.sum(grad_rows.astype(f32) * expert_out, axis=4)
     send_back = slot_part.reshape(block_count, local_count, capacity)
     returned = lax.all_to_all(
         send_back, ("expert", "dp"), split_axis=0, concat_axis=0, tiled=True
     )
     returned = returned.reshape(peer_count, shards, local_count, capacity)
-    slot_grad = jnp.sum(returned, axis=1).reshape(expert_count * capacity)
+    slot_grad = jnp.sum(returned, axis=1).reshape(expert_count, capacity)
 
-    own_chose = jnp.any(
-        expert_ids[:, :, None] == jnp.arange(expert_count, dtype=jnp.int32)[None, None, :], axis=1
-    )
+    own_hit = expert_ids[:, :, None] == jnp.arange(expert_count, dtype=jnp.int32)[None, None, :]
+    own_chose = jnp.any(own_hit, axis=1)
     own_rank = jnp.einsum(
         "ue,ut->te", own_chose.astype(bf16), before, preferred_element_type=f32
     ).astype(jnp.int32)
-    own_slot = jnp.take_along_axis(own_rank, expert_ids, axis=1)
-    gate_grad = slot_grad[expert_ids * capacity + own_slot]
+    own_slot = jnp.sum(jnp.where(own_hit, own_rank[:, None, :], 0), axis=2)
+    by_slot = jnp.sum(jnp.where(own_hit[:, :, :, None], slot_grad[None, None], 0.0), axis=2)
+    gate_grad = jnp.sum(
+        jnp.where(own_slot[:, :, None] == slot_ids[None, None, :], by_slot, 0.0), axis=2
+    )
     return (weight_grad, gate_grad)
 
 

time: 190 us -> 152 us (0.80)
  blocking collectives: 52.1 us -> 13.3 us
  other arithmetic: 1.04 us -> 7.75 us
  waiting for transfers between devices: 37.1 us -> 43.6 us
  local copies, waits for them, and re-layouts: 38.8 us -> 32.5 us
  matrix products: 41.3 us -> 35.5 us
    ppermute x0 -> x2, waiting for transfers between devices: none -> 39.3 us  [the longest x1 39.3 us: per_device(): fetched = lax.ppermute(hidden, 'dp', [(j, j ^ 2) for j in range(shards)])]
    all_gather x2 -> x0, blocking collectives: 39.3 us -> none  [the longest x1 21.2 us: per_device(): lax.all_gather(gate_weights, ('expert', 'dp'), axis=0, tiled=True)]
    all_gather x2 -> x1, waiting for transfers between devices: 37 us -> 4.34 us  [per_device(): got = lax.all_gather(cols, 'expert', axis=0, tiled=False)]
    gather x7 -> x0, local copies, waits for them, and re-layouts: 13.6 us -> none  [the longest x5 7.34 us: per_device(): own_slot = jnp.take_along_axis(own_rank, expert_ids, axis=1)]
    dot_general x1, matrix products: 6.05 us -> 1.51 us  [per_device(): jnp.einsum('blct,btd->blcd', select.astype(bf16), grad_all, preferred_ele...]
    dynamic_slice x0 -> x1, local copies, waits for them, and re-layouts: none -> 4.08 us  [per_device(): lax.dynamic_index_in_dim(grad_rows, replica, axis=1, keepdims=False)]
    concatenate x0 -> x3, other arithmetic: none -> 3.2 us  [the longest x1 2.31 us: per_device(): jnp.concatenate([hidden, fetched], axis=1)]
    dynamic_update_slice x0 -> x4, local copies, waits for them, and re-layouts: none -> 2.43 us  [per_device(): lax.dynamic_update_index_in_dim(slot_part, slot_r, replica, axis=1)]
  transfers between devices with their start and end apart: 3 -> 4, of which waited for: 1 -> 2; matrix products, arithmetic and copies ran while one was open for 31% -> 39% of each run, Pallas kernels for 0% -> 0%
where the time goes in v2:
time: 152 us
  waiting for transfers between devices  43.6 us (29%)
  matrix products  35.5 us (23%)
  local copies, waits for them, and re-layouts  32.5 us (21%)
  between operations  14.3 us (9%)
  blocking collectives  13.3 us (9%)
  other arithmetic  7.75 us (5%)
  starting transfers between devices  4.59 us (3%)
    ppermute x1, waiting for transfers between devices, per_device(): fetched = lax.ppermute(hidden, 'dp', [(j, j ^ 2) for j in range(shards)])  39.3 us
    dot_general x4, matrix products, per_device(): jnp.einsum('lscf,slcd->lfd', piece, scaled_r, preferred_element_type=f32)  19.4 us
    unnamed x37, local copies, waits for them, and re-layouts  19.2 us
    all_to_all x1, blocking collectives, per_device(): cols = lax.all_to_all(cols, 'dp', split_axis=1, concat_axis=0, tiled=True)  13.3 us
    dot_general x4, matrix products, per_device(): jnp.einsum('lscf,lfd->slcd', piece, down_weight, preferred_element_type=f32)  12.7 us
    all_gather x1, waiting for transfers between devices, per_device(): got = lax.all_gather(cols, 'expert', axis=0, tiled=False)  4.34 us
    all_to_all x1, starting transfers between devices, per_device(): lax.all_to_all(send_back, ('expert', 'dp'), split_axis=0, concat_axis=0,...  4.13 us
    dynamic_slice x1, local copies, waits for them, and re-layouts, per_device(): lax.dynamic_index_in_dim(grad_rows, replica, axis=1, keepdims=False)  4.08 us
  transfers between devices with their start and end apart: 4, of which 2 were waited for; matrix products, arithmetic and copies ran while one was open for 39% of the time, Pallas kernels for 0%

profile of v2, /device:TPU:0, one launch (start us, length us, event | category | flops | bytes accessed | tf_op | source)
XLA Modules:
  0.0 151.6 jit_solution(17778870522974405558)
XLA Ops:
  7.2 0.7 convert_element_type.81
  7.9 0.7 pad_maximum_fusion.2
  8.6 0.1 copy.187
  8.8 0.2 copy.188
  9.0 1.3 copy.186
  10.4 0.2 pad_maximum_fusion.1
  10.6 0.5 copy.189
  11.1 13.3 %all_to_all.20 = bf16[132,4,512]{2,0,1:T(8,128)(2,1)} all-to-all(bf16[132,4,512]{2,0,1:T(8,128)(2,1)S(1)} %copy.189), channel_id=1, replica_groups=mesh['groups'=2,'expert'=4,'dp'=4] {'dp'}, dimensions={1} | all-to-all | bytes 1081344 | tf_op jit(solution)/shard_map/all_to_all | solution.py:34
  24.4 2.0 %copy.196 = bf16[8,1,4,36,768]{4,0,3,2,1:T(8,128)(2,1)S(1)} copy(bf16[8,1,4,36,768]{4,2,3,1,0:T(4,128)(2,1)} %param.8) | data formatting | bytes 3538944 | tf_op args[3]
  26.4 0.4 collective-permute-start
  26.9 0.6 fusion.51
  27.5 0.1 convolution_convert_fusion.3
  27.7 39.3 %collective-permute-done = bf16[8,1,4,36,768]{4,0,3,2,1:T(8,128)(2,1)S(1)} collective-permute-done((bf16[8,1,4,36,768]{4,0,3,2,1:T(8,128)(2,1)S(1)}, bf16[8,1,4,36,768]{4,0,3,2,1:T(8,128)(2,1)S(1)}, u32[]{:S(2)}, u32[]{:S(2)}) %collective-permute-start) | collective-permute-done | bytes 1769504 | tf_op jit(solution)/shard_map/ppermute | solution.py:21
  67.0 2.3 %pad_maximum_fusion = bf16[8,2,4,36,768]{4,0,3,2,1:T(8,128)(2,1)} fusion(bf16[8,1,4,36,768]{4,0,3,2,1:T(8,128)(2,1)S(1)} %collective-permute-done, bf16[8,1,4,36,768]{4,0,3,2,1:T(8,128)(2,1)S(1)} %copy.196), kind=kLoop, calls=%fused_computation.15 | loop fusion | flops 1769472 | bytes 7077888 | tf_op jit(solution)/shard_map/concatenate | solution.py:23
  69.3 4.3 %all-gather.3.cloned.1.call-done = bf16[16,132,1,512]{3,1,2,0:T(8,128)(2,1)} async-done(((bf16[4,132,1,512]{3,1,2,0:T(8,128)(2,1)}), bf16[16,132,1,512]{3,1,2,0:T(8,128)(2,1)}) %all-gather.3.cloned.1.call-update) | async-done | bytes 2162704 | tf_op jit(solution)/shard_map/all_gather | solution.py:36
  73.7 0.9 slice.24
  74.6 0.4 reshape_reshape.3
  75.0 1.0 fusion.56
  76.0 1.2 copy.226
  77.2 0.2 copy.233
  77.4 0.1 compare_reduce_fusion
  77.6 0.1 fusion.50
  77.7 0.1 convolution_convert_fusion.2
  77.9 1.5 convolution_convert_fusion.1
  79.4 0.1 copy-done.2
  79.5 1.5 %convolution_convert_fusion = bf16[16,8,36,512]{3,2,1,0:T(8,128)(2,1)S(1)} fusion(bf16[16,132,512]{2,1,0:T(8,128)(2,1)S(1)} %bitcast.135, bf16[16,8,128]{2,1,0:T(8,128)(2,1)S(1)} %bitcast.142, s32[16,8,128]{2,1,0:T(8,128)S(1)} %convolution_convert_fusion.2, pred[16,8,128]{2,1,0:T(8,128)(4,1)S(1)} %bitcast.141), kind=kOutput, calls=%fused_computation.16 | convolution fusion | flops 608108544 | bytes 6930432 | tf_op jit(solution)/shard_map/blct,btd->blcd/dot_general | solution.py:61
  81.0 4.1 %constant_dynamic-slice_fusion = (bf16[4,1,8,36,512]{4,3,2,1,0:T(8,128)(2,1)}, bf16[4,1,8,36,512]{4,3,2,1,0:T(8,128)(2,1)}, bf16[4,1,8,36,512]{4,3,2,1,0:T(8,128...) fusion(bf16[4,4,8,36,512]{4,3,2,1,0:T(8,128)(2,1)S(1)} %bitcast, ...), kind=kLoop, calls=%fused_computation.78 | loop fusion | bytes 18874384 | tf_op jit(solution)/shard_map/jit(dynamic_index_in_dim)/dynamic_slice | solution.py:72
  85.1 5.0 %fusion.12 = f32[4,8,36]{2,0,1:T(4,128)S(1)} fusion(bf16[4,1,8,36,512]{4,3,2,1,0:T(8,128)(2,1)} %get-tuple-element.21, bf16[8,4,36,768]{3,1,2,0:T(4,128)(2,1)} %bitcast.138, bf16[8,768,512]{2,1,0:T(8,128)(2,1)} %param.9), kind=kOutput, calls=%fused_computation.25 | convolution fusion | flops 907737984 | bytes 9245184 | tf_op jit(solution)/shard_map/lscf,lfd->slcd/dot_general | solution.py:77
  90.2 0.6 broadcast_in_dim.109
  90.8 0.6 copy_dynamic-update-slice_fusion.3
  91.4 4.3 %fusion.11 = f32[4,8,36]{2,0,1:T(4,128)S(1)} fusion(bf16[4,1,8,36,512]{4,3,2,1,0:T(8,128)(2,1)S(1)} %copy-done.10, bf16[8,1,4,36,768]{4,0,3,2,1:T(8,128)(2,1)S(1)} %copy-done.4, bf16[8,768,512]{2,1,0:T(8,128)(2,1)} %param.9), kind=kOutput, calls=%fused_computation.23 | convolution fusion | flops 907737984 | bytes 9245184 | tf_op jit(solution)/shard_map/lscf,lfd->slcd/dot_general | solution.py:77
  95.7 0.6 copy_dynamic-update-slice_fusion.2
  96.4 4.6 %fusion.22 = bf16[8,512,768,1]{2,1,3,0:T(8,128)(2,1)} fusion(bf16[8,4,36,768]{3,1,2,0:T(4,128)(2,1)S(1)} %bitcast.139, bf16[4,1,8,36,512]{4,3,2,1,0:T(8,128)(2,1)S(1)} %copy-done.9), kind=kOutput, calls=%fused_computation.39 | convolution fusion | flops 905969664 | bytes 9240576 | tf_op jit(solution)/shard_map/lscf,slcd->lfd/dot_general | solution.py:73
  101.0 2.3 %fusion.55 = (bf16[8,1,4,36,768]{4,0,3,2,1:T(8,128)(2,1)S(1)}, bf16[8,1,4,36,768]{4,0,3,2,1:T(8,128)(2,1)S(1)}) fusion(bf16[8,2,4,36,768]{4,0,3,2,1:T(8,128)(2,1)} %collective-permute-done.1), kind=kLoop, calls=%fused_computation.88 | loop fusion | bytes 7077888 | tf_op jit(solution)/shard_map/slice | solution.py:25
  103.4 1.6 %fusion.9 = f32[4,8,36]{2,0,1:T(4,128)S(1)} fusion(bf16[4,1,8,36,512]{4,3,2,1,0:T(8,128)(2,1)S(1)} %copy-done.8, bf16[8,768,512]{2,1,0:T(8,128)(2,1)S(1)} %bitcast.149, bf16[8,1,4,36,768]{4,0,3,2,1:T(8,128)(2,1)S(1)} %get-tuple-element.26), kind=kOutput, calls=%fused_computation.19 | convolution fusion | flops 907737984 | bytes 9245184 | tf_op jit(solution)/shard_map/lscf,lfd->slcd/dot_general | solution.py:77
  105.0 1.8 %fusion.10 = f32[4,8,36]{2,0,1:T(4,128)S(1)} fusion(bf16[4,1,8,36,512]{4,3,2,1,0:T(8,128)(2,1)S(1)} %copy-done.7, bf16[8,768,512]{2,1,0:T(8,128)(2,1)S(1)} %bitcast.149, bf16[8,1,4,36,768]{4,0,3,2,1:T(8,128)(2,1)S(1)} %get-tuple-element.27), kind=kOutput, calls=%fused_computation.21 | convolution fusion | flops 907737984 | bytes 9245184 | tf_op jit(solution)/shard_map/lscf,lfd->slcd/dot_general | solution.py:77
  106.8 0.6 copy_dynamic-update-slice_fusion.1
  107.4 0.6 copy_dynamic-update-slice_fusion
  108.0 1.6 %reshape.70 = f32[16,1,288]{2,1,0:T(1,128)} reshape(f32[16,8,36]{2,1,0:T(8,128)} %bitcast.43) | data formatting | bytes 36864
  109.5 4.1 %all-to-all-start.1 = ((f32[16,1,288]{2,1,0:T(1,128)}), f32[16,1,288]{2,1,0:T(1,128)}, u32[]{:S(2)}, u32[]{:S(2)}) async-start(f32[16,1,288]{2,1,0:T(1,128)} %reshape.70), calls=%async_computation.1 | async-start | bytes 49152 | tf_op jit(solution)/shard_map/all_to_all | solution.py:84
  113.7 3.4 %fusion.17 = bf16[8,768,512,1]{1,2,3,0:T(8,128)(2,1)S(1)} fusion(bf16[8,1,4,36,768]{4,0,3,2,1:T(8,128)(2,1)S(1)} %get-tuple-element.27, bf16[4,1,8,36,512]{4,3,2,1,0:T(8,128)(2,1)} %get-tuple-element.33), kind=kOutput, calls=%fused_computation.34 | convolution fusion | flops 905969664 | bytes 9240576 | tf_op jit(solution)/shard_map/lscf,slcd->lfd/dot_general | solution.py:73
  117.1 1.9 %fusion.18 = bf16[8,768,512,1]{1,2,3,0:T(8,128)(2,1)S(1)} fusion(bf16[8,1,4,36,768]{4,0,3,2,1:T(8,128)(2,1)S(1)} %get-tuple-element.26, bf16[4,1,8,36,512]{4,3,2,1,0:T(8,128)(2,1)S(1)} %copy-done), kind=kOutput, calls=%fused_computation.35 | convolution fusion | flops 905969664 | bytes 9240576 | tf_op jit(solution)/shard_map/lscf,slcd->lfd/dot_general | solution.py:73
  119.0 9.5 %fusion = f32[8,768,512]{1,2,0:T(8,128)} fusion(bf16[8,512,768,1]{2,1,3,0:T(8,128)(2,1)} %fusion.22, bf16[8,768,512,1]{1,2,3,0:T(8,128)(2,1)S(1)} %fusion.17, bf16[8,768,512,1]{1,2,3,0:T(8,128)(2,1)S(1)} %fusion.18, bf16[8,1,4,36,768]{4,0,3,2,1:T(8,128)(2,1)S(1)} %copy-done.5, bf16[4,1,8,36,512]{4,3,2,1,0:T(8,128)(2,1)} %get-tuple-element.35), kind=kOutput, calls=%fused_computation.3 | convolution fusion | flops 931135488 | bytes 34406400 | tf_op jit(solution)/shard_map/lscf,slcd->lfd/dot_general | solution.py:73
  128.5 12.6 %copy.216 = f32[8,768,512]{2,1,0:T(8,128)} copy(f32[8,768,512]{1,2,0:T(8,128)} %fusion) | data formatting | bytes 25165824
  141.1 0.5 broadcast.17
  141.6 1.4 reduce
  143.3 0.8 select_reduce_fusion
  144.1 0.6 select_reduce_fusion.1
  (44 shorter events, 0.6 us)
Async XLA Ops:
  7.2 66.5 %all-gather.3.cloned.1.call-start = ((), (), s32[]{:S(2)}) async-start(), calls=%async_computation.2 | async-start | bytes 2785280 | tf_op jit(solution)/shard_map/all_gather | solution.py:36
  24.4 2.5 %copy-start.12 = (s32[128,8]{0,1:T(8,128)S(1)}, s32[128,8]{0,1:T(8,128)}, u32[]{:S(2)}) copy-start(s32[128,8]{0,1:T(8,128)} %param.7) | copy-start | bytes 12292
  26.4 40.5 %collective-permute-start = (bf16[8,1,4,36,768]{4,0,3,2,1:T(8,128)(2,1)S(1)}, bf16[8,1,4,36,768]{4,0,3,2,1:T(8,128)(2,1)S(1)}, u32[]{:S(2)}, u32[]{:S(2)}) collective-permute-start(bf16[8,1,4,36,768]{4,0,3,2,1:T(8,128)(2,1)S(1)} %copy.196), channel_id=1, source_target_pairs={{0,2},{1,3},{2,0},{3,1},{4,6},{5,7},{6,4},{7,5},{8,10},{9,11},{10,... | collective-permute-start | bytes 5308424 | tf_op jit(solution)/shard_map/ppermute | solution.py:21
  67.0 2.4 %copy-start.3 = (bf16[8,1,4,36,768]{4,0,3,2,1:T(8,128)(2,1)}, bf16[8,1,4,36,768]{4,0,3,2,1:T(8,128)(2,1)S(1)}, u32[]{:S(2)}) copy-start(bf16[8,1,4,36,768]{4,0,3,2,1:T(8,128)(2,1)S(1)} %collective-permute-done) | copy-start | bytes 5308420
  69.3 31.7 %collective-permute-start.1 = (bf16[8,2,4,36,768]{4,0,3,2,1:T(8,128)(2,1)}, bf16[8,2,4,36,768]{4,0,3,2,1:T(8,128)(2,1)}, u32[]{:S(2)}, u32[]{:S(2)}) collective-permute-start(bf16[8,2,4,36,768]{4,0,3,2,1:T(8,128)(2,1)} %pad_maximum_fusion), channel_id=1, source_target_pairs={{0,1},{1,0},{2,3},{3,2},{4,5},{5,4},{6,7},{7,6},{8,9},{9,8},{10,11... | collective-permute-start | bytes 10616840 | tf_op jit(solution)/shard_map/ppermute | solution.py:22
  75.0 2.9 %copy-start.1 = (bf16[16,132,1,512]{3,1,2,0:T(8,128)(2,1)S(1)}, bf16[16,132,1,512]{3,1,2,0:T(8,128)(2,1)}, u32[]{:S(2)}) copy-start(bf16[16,132,1,512]{3,1,2,0:T(8,128)(2,1)} %all-gather.3.cloned.1.call-done) | copy-start | bytes 6488068
  77.9 1.6 %copy-start.2 = (bf16[16,132,1,512]{3,1,2,0:T(8,128)(2,1)S(1)}, bf16[16,132,1,512]{3,1,2,0:T(8,128)(2,1)}, u32[]{:S(2)}) copy-start(bf16[16,132,1,512]{3,1,2,0:T(8,128)(2,1)} %all-gather.3.cloned.1.call-done) | copy-start | bytes 6488068
  85.1 6.3 %copy-start.4 = (bf16[8,1,4,36,768]{4,0,3,2,1:T(8,128)(2,1)S(1)}, bf16[8,1,4,36,768]{4,0,3,2,1:T(8,128)(2,1)}, u32[]{:S(2)}) copy-start(bf16[8,1,4,36,768]{4,0,3,2,1:T(8,128)(2,1)} %copy-done.3) | copy-start | bytes 5308420
  85.1 6.3 %copy-start.10 = (bf16[4,1,8,36,512]{4,3,2,1,0:T(8,128)(2,1)S(1)}, bf16[4,1,8,36,512]{4,3,2,1,0:T(8,128)(2,1)}, u32[]{:S(2)}) copy-start(bf16[4,1,8,36,512]{4,3,2,1,0:T(8,128)(2,1)} %get-tuple-element.20) | copy-start | bytes 3538948
  91.4 5.0 %copy-start.6 = (bf16[8,1,4,36,768]{4,2,3,1,0:T(4,128)(2,1)S(1)}, bf16[8,1,4,36,768]{4,2,3,1,0:T(4,128)(2,1)}, u32[]{:S(2)}) copy-start(bf16[8,1,4,36,768]{4,2,3,1,0:T(4,128)(2,1)} %param.8) | copy-start | bytes 5308420
  91.4 5.0 %copy-start.9 = (bf16[4,1,8,36,512]{4,3,2,1,0:T(8,128)(2,1)S(1)}, bf16[4,1,8,36,512]{4,3,2,1,0:T(8,128)(2,1)}, u32[]{:S(2)}) copy-start(bf16[4,1,8,36,512]{4,3,2,1,0:T(8,128)(2,1)} %get-tuple-element.32) | copy-start | bytes 3538948
  91.4 12.0 %slice-start = ((s8[6291456]{0:T(1024)(128)(4,1)}), s8[2097152]{0:T(1024)(128)(4,1)S(1)}, s32[]{:S(2)}) async-start(s8[6291456]{0:T(1024)(128)(4,1)} %bitcast.148), calls=%async_computation.3 | async-start | bytes 4194304
  96.4 7.0 %slice-start.1 = ((s8[6291456]{0:T(1024)(128)(4,1)}), s8[4194304]{0:T(1024)(128)(4,1)S(1)}, s32[]{:S(2)}) async-start(s8[6291456]{0:T(1024)(128)(4,1)} %bitcast.148), calls=%async_computation.4 | async-start | bytes 8388608
  101.0 2.4 %copy-start.8 = (bf16[4,1,8,36,512]{4,3,2,1,0:T(8,128)(2,1)S(1)}, bf16[4,1,8,36,512]{4,3,2,1,0:T(8,128)(2,1)}, u32[]{:S(2)}) copy-start(bf16[4,1,8,36,512]{4,3,2,1,0:T(8,128)(2,1)} %get-tuple-element.18) | copy-start | bytes 3538948
  103.4 1.6 %copy-start.7 = (bf16[4,1,8,36,512]{4,3,2,1,0:T(8,128)(2,1)S(1)}, bf16[4,1,8,36,512]{4,3,2,1,0:T(8,128)(2,1)}, u32[]{:S(2)}) copy-start(bf16[4,1,8,36,512]{4,3,2,1,0:T(8,128)(2,1)} %get-tuple-element.19) | copy-start | bytes 3538948
  109.5 31.6 %all-to-all-start.1 = ((f32[16,1,288]{2,1,0:T(1,128)}), f32[16,1,288]{2,1,0:T(1,128)}, u32[]{:S(2)}, u32[]{:S(2)}) async-start(f32[16,1,288]{2,1,0:T(1,128)} %reshape.70), calls=%async_computation.1 | async-start | bytes 49152 | tf_op jit(solution)/shard_map/all_to_all | solution.py:84
  113.7 3.4 %copy-start = (bf16[4,1,8,36,512]{4,3,2,1,0:T(8,128)(2,1)S(1)}, bf16[4,1,8,36,512]{4,3,2,1,0:T(8,128)(2,1)}, u32[]{:S(2)}) copy-start(bf16[4,1,8,36,512]{4,3,2,1,0:T(8,128)(2,1)} %get-tuple-element.34) | copy-start | bytes 3538948
  117.1 2.0 %copy-start.5 = (bf16[8,1,4,36,768]{4,0,3,2,1:T(8,128)(2,1)S(1)}, bf16[8,1,4,36,768]{4,0,3,2,1:T(8,128)(2,1)}, u32[]{:S(2)}) copy-start(bf16[8,1,4,36,768]{4,0,3,2,1:T(8,128)(2,1)} %copy-done.3) | copy-start | bytes 5308420
  128.5 14.8 %copy-start.11 = (pred[128,8,32]{0,2,1:T(8,128)(4,1)S(1)}, pred[128,8,32]{0,2,1:T(8,128)(4,1)}, u32[]{:S(2)}) copy-start(pred[128,8,32]{0,2,1:T(8,128)(4,1)} %get-tuple-element.31) | copy-start | bytes 98308
Sparse Core Ops, SparseCore 0:
  24.6 49.0 all-gather.2

commit v3 on v2

--- a/solution.py
+++ b/solution.py
@@ -1,7 +1,56 @@
 import jax
 import jax.numpy as jnp
 from jax import lax
+from jax.experimental import pallas as pl
 from jax.sharding import PartitionSpec as P
+
+
+def expert_body(h_ref, s_ref, g_ref, w_ref, wg_ref, slot_ref):
+    chunk = pl.program_id(1)
+    h = h_ref[0]
+    part = lax.dot_general(
+        h, s_ref[0], (((0,), (0,)), ((), ())), preferred_element_type=jnp.float32
+    )
+
+    @pl.when(chunk == 0)
+    def _():
+        wg_ref[0] = part
+
+    @pl.when(chunk != 0)
+    def _():
+        wg_ref[0] = wg_ref[0] + part
+
+    out = jnp.dot(h, w_ref[0], preferred_element_type=jnp.float32)
+    slot_ref[0] = jnp.sum(g_ref[0].astype(jnp.float32) * out, axis=1, keepdims=True)
+
+
+def expert_kernel(hidden_rows, scaled_rows, grad_rows, weight):
+    local_count, slot_rows, hidden_width = hidden_rows.shape
+    col_width = scaled_rows.shape[2]
+    chunk = slot_rows
+    for size in (576, 512, 384, 256, 128):
+        if slot_rows % size == 0:
+            chunk = size
+            break
+    steps = slot_rows // chunk
+    return pl.pallas_call(
+        expert_body,
+        grid=(local_count, steps),
+        in_specs=[
+            pl.BlockSpec((1, chunk, hidden_width), lambda l, r: (l, r, 0)),
+            pl.BlockSpec((1, chunk, col_width), lambda l, r: (l, r, 0)),
+            pl.BlockSpec((1, chunk, col_width), lambda l, r: (l, r, 0)),
+            pl.BlockSpec((1, hidden_width, col_width), lambda l, r: (l, 0, 0)),
+        ],
+        out_specs=[
+            pl.BlockSpec((1, hidden_width, col_width), lambda l, r: (l, 0, 0)),
+            pl.BlockSpec((1, chunk, 1), lambda l, r: (l, r, 0)),
+        ],
+        out_shape=[
+            jax.ShapeDtypeStruct((local_count, hidden_width, col_width), jnp.float32),
+            jax.ShapeDtypeStruct((local_count, slot_rows, 1), jnp.float32),
+        ],
+    )(hidden_rows, scaled_rows, grad_rows, weight)
 
 
 def per_device(out_grad, gate_weights, expert_ids, hidden, down_weight):
@@ -9,6 +58,7 @@
     row_width = out_grad.shape[1]
     local_count = hidden.shape[0]
     capacity = hidden.shape[3]
+    hidden_width = hidden.shape[4]
     peer_count = lax.axis_size("expert")
     shards = lax.axis_size("dp")
     expert_count = local_count * peer_count
@@ -64,22 +114,15 @@
     grad_rows = grad_rows.reshape(peer_count, shards, local_count, capacity, col_width)
     scaled = scaled.reshape(peer_count, shards, local_count, capacity, col_width)
 
-    weight_grad = None
-    slot_part = jnp.zeros((peer_count, shards, local_count, capacity), f32)
-    for piece, replica in zip(pieces, piece_replica):
-        piece = piece[:, 0]
-        scaled_r = lax.dynamic_index_in_dim(scaled, replica, axis=1, keepdims=False)
-        rows_r = lax.dynamic_index_in_dim(grad_rows, replica, axis=1, keepdims=False)
-        part = jnp.einsum(
-            "lscf,slcd->lfd", piece, scaled_r, preferred_element_type=f32
-        ).astype(bf16).astype(f32)
-        weight_grad = part if weight_grad is None else weight_grad + part
-        expert_out = jnp.einsum(
-            "lscf,lfd->slcd", piece, down_weight, preferred_element_type=f32
-        )
-        slot_r = jnp.sum(rows_r.astype(f32) * expert_out, axis=3)
-        slot_part = lax.dynamic_update_index_in_dim(slot_part, slot_r, replica, axis=1)
-
+    hidden_all = jnp.concatenate([hidden, fetched, paired], axis=1)
+    piece_of = jnp.array([0, 2, 1, 3], jnp.int32)[jnp.arange(shards, dtype=jnp.int32) ^ my_dp]
+    hidden_all = jnp.take(hidden_all, piece_of, axis=1)
+    slot_rows = shards * peer_count * capacity
+    hidden_rows = hidden_all.reshape(local_count, slot_rows, hidden_width)
+    scaled_rows = scaled.transpose(2, 1, 0, 3, 4).reshape(local_count, slot_rows, col_width)
+    grad_slot_rows = grad_rows.transpose(2, 1, 0, 3, 4).reshape(local_count, slot_rows, col_width)
+    weight_grad, slot_part = expert_kernel(hidden_rows, scaled_rows, grad_slot_rows, down_weight)
+    slot_part = slot_part.reshape(local_count, shards, peer_count, capacity).transpose(2, 1, 0, 3)
     send_back = slot_part.reshape(block_count, local_count, capacity)
     returned = lax.all_to_all(
         send_back, ("expert", "dp"), split_axis=0, concat_axis=0, tiled=True

time: 152 us -> 198 us (1.30)
  matrix products: 35.5 us -> 5.52 us
  blocking collectives: 13.3 us -> 34.9 us
  other arithmetic: 7.75 us -> 28.5 us
  Pallas kernels: 0 us -> 15.8 us
  local copies, waits for them, and re-layouts: 32.5 us -> 40.4 us
  waiting for transfers between devices: 43.6 us -> 51.2 us
  starting transfers between devices: 4.59 us -> 6.57 us
    all_gather x1, waiting for transfers between devices: 4.34 us -> 44.6 us  [per_device(): got = lax.all_gather(cols, 'expert', axis=0, tiled=False)]
    ppermute x1, waiting for transfers between devices: 39.3 us -> 0.01 us  [per_device(): fetched = lax.ppermute(hidden, 'dp', [(j, j ^ 2) for j in range(shards)])]
    dot_general x8 -> x0, matrix products: 32.2 us -> none  [the longest x4 19.4 us: per_device(): jnp.einsum('lscf,slcd->lfd', piece, scaled_r, preferred_element_type=f32)]
    all_to_all x1, blocking collectives: 13.3 us -> 34.9 us  [per_device(): cols = lax.all_to_all(cols, 'dp', split_axis=1, concat_axis=0, tiled=True)]
    pallas_call x0 -> x1, Pallas kernels: none -> 15.8 us  [expert_kernel(): pl.pallas_call(expert_body, grid=(local_count, steps), in_specs=[pl.Block...]
    reshape x0 -> x5, local copies, waits for them, and re-layouts: none -> 11.8 us  [the longest x1 3.97 us: per_device(): grad_rows.transpose(2, 1, 0, 3, 4)]
    unnamed x37 -> x20, local copies, waits for them, and re-layouts: 19.2 us -> 8.8 us
    select_n x0 -> x3, other arithmetic: none -> 9.38 us  [the longest x2 9.38 us: per_device(): hidden_all = jnp.take(hidden_all, piece_of, axis=1)]
  transfers between devices with their start and end apart: 4 -> 4, of which waited for: 2 -> 2; matrix products, arithmetic and copies ran while one was open for 39% -> 23% of each run, Pallas kernels for 0% -> 0%
where the time goes in v3:
time: 198 us; the launch traced here: 197 us
  waiting for transfers between devices  51.2 us (26%)
  local copies, waits for them, and re-layouts  40.4 us (20%)
  blocking collectives  34.9 us (18%)
  other arithmetic  28.5 us (14%)
  Pallas kernels  15.8 us (8%)
  between operations  14.2 us (7%)
  starting transfers between devices  6.57 us (3%)
  matrix products  5.52 us (3%)
    all_gather x1, waiting for transfers between devices, per_device(): got = lax.all_gather(cols, 'expert', axis=0, tiled=False)  44.6 us
    all_to_all x1, blocking collectives, per_device(): cols = lax.all_to_all(cols, 'dp', split_axis=1, concat_axis=0, tiled=True)  34.9 us
    pallas_call x1, Pallas kernels, expert_kernel(): pl.pallas_call(expert_body, grid=(local_count, steps), in_specs=[pl.Block...  15.8 us
    select_n x2, other arithmetic, per_device(): hidden_all = jnp.take(hidden_all, piece_of, axis=1)  9.38 us
    unnamed x20, local copies, waits for them, and re-layouts  8.8 us
    gather x1, local copies, waits for them, and re-layouts, per_device(): hidden_all = jnp.take(hidden_all, piece_of, axis=1)  6.95 us
    all_to_all x1, waiting for transfers between devices, per_device(): lax.all_to_all(send_back, ('expert', 'dp'), split_axis=0, concat_axis=0,...  6.52 us
    concatenate x1, other arithmetic, per_device(): hidden_all = jnp.concatenate([hidden, fetched, paired], axis=1)  5.49 us
  transfers between devices with their start and end apart: 4, of which 2 were waited for; matrix products, arithmetic and copies ran while one was open for 23% of the time, Pallas kernels for 0%

profile of v3, /device:TPU:0, one launch (start us, length us, event | category | flops | bytes accessed | tf_op | source)
XLA Modules:
  0.0 197.2 jit_solution(14552400161750992420)
XLA Ops:
  7.2 2.0 %copy.106 = bf16[8,1,4,36,768]{4,0,3,2,1:T(8,128)(2,1)S(1)} copy(bf16[8,1,4,36,768]{4,2,3,1,0:T(4,128)(2,1)} %param.9) | data formatting | bytes 3538944 | tf_op args[3]
  9.2 3.0 %collective-permute-start = (bf16[8,1,4,36,768]{4,0,3,2,1:T(8,128)(2,1)S(1)}, bf16[8,1,4,36,768]{4,0,3,2,1:T(8,128)(2,1)S(1)}, u32[]{:S(2)}, u32[]{:S(2)}) collective-permute-start(bf16[8,1,4,36,768]{4,0,3,2,1:T(8,128)(2,1)S(1)} %copy.106), channel_id=1, source_target_pairs={{0,2},{1,3},{2,0},{3,1},{4,6},{5,7},{6,4},{7,5},{8,10},{9,11},{10,... | collective-permute-start | bytes 5308424 | tf_op jit(solution)/shard_map/ppermute | solution.py:71
  12.3 0.7 copy.109
  13.0 0.9 broadcast_in_dim.103
  13.8 0.8 copy.110
  14.7 2.0 %copy.108 = bf16[128,2048]{0,1:T(8,128)(2,1)} copy(bf16[128,2048]{1,0:T(8,128)(2,1)} %param.6) | data formatting | bytes 1048576 | tf_op args[0]
  16.7 1.0 broadcast_in_dim.104
  17.7 2.2 %pad_maximum_fusion.2 = bf16[132,4,512]{0,2,1:T(8,128)(2,1)} fusion(bf16[4,4,512]{0,2,1:T(8,128)(2,1)S(1)} %broadcast_in_dim.104, bf16[128,4,512]{0,2,1:T(8,128)(2,1)} %bitcast.51), kind=kLoop, calls=%fused_computation.20 | loop fusion | flops 1081344 | bytes 1081344 | tf_op jit(solution)/shard_map/concatenate | solution.py:83
  19.9 2.1 %copy.111 = bf16[132,4,512]{2,0,1:T(8,128)(2,1)} copy(bf16[132,4,512]{0,2,1:T(8,128)(2,1)} %pad_maximum_fusion.2) | data formatting | bytes 1081344 | tf_op jit(solution)/shard_map/concatenate | solution.py:83
  22.0 34.9 %all_to_all.20 = bf16[132,4,512]{2,0,1:T(8,128)(2,1)} all-to-all(bf16[132,4,512]{2,0,1:T(8,128)(2,1)} %copy.111), channel_id=1, replica_groups=mesh['groups'=2,'expert'=4,'dp'=4] {'dp'}, dimensions={1} | all-to-all | bytes 1081344 | tf_op jit(solution)/shard_map/all_to_all | solution.py:84
  57.0 2.1 %pad_maximum_fusion.1 = bf16[8,2,4,36,768]{4,0,3,2,1:T(8,128)(2,1)} fusion(bf16[8,1,4,36,768]{4,0,3,2,1:T(8,128)(2,1)S(1)} %collective-permute-done, bf16[8,1,4,36,768]{4,0,3,2,1:T(8,128)(2,1)S(1)} %copy.106), kind=kLoop, calls=%fused_computation.5 | loop fusion | flops 1769472 | bytes 7077888 | tf_op jit(solution)/shard_map/concatenate | solution.py:73
  59.1 0.6 gather_fusion
  59.8 0.1 broadcast_in_dim.100
  59.9 0.3 copy-done.6
  60.3 0.7 fusion.13
  60.9 0.6 fusion.9
  61.5 0.7 convolution_convert_fusion.3
  62.3 44.6 %all-gather.3.cloned.1.call-done = bf16[16,132,1,512]{3,1,2,0:T(8,128)(2,1)} async-done(((bf16[4,132,1,512]{3,1,2,0:T(8,128)(2,1)}), bf16[16,132,1,512]{3,1,2,0:T(8,128)(2,1)}) %all-gather.3.cloned.1.call-update) | async-done | bytes 2162704 | tf_op jit(solution)/shard_map/all_gather | solution.py:86
  106.9 1.5 slice.20
  108.5 2.0 %reshape_reshape.3 = bf16[16,128,16]{2,1,0:T(8,128)(2,1)} reshape(bf16[16,4,512]{2,1,0:T(4,128)(2,1)} %slice.20) | data formatting | bytes 131072 | tf_op jit(solution)/shard_map/reshape;reshape | solution.py:90
  110.5 2.4 %fusion.15 = (bf16[16,128,8]{2,1,0:T(8,128)(2,1)}, bf16[16,128,8]{2,1,0:T(8,128)(2,1)}) fusion(bf16[16,128,16]{2,1,0:T(8,128)(2,1)} %reshape_reshape.3), kind=kLoop, calls=%fused_computation.43 | loop fusion | bytes 131072 | tf_op jit(solution)/shard_map/slice | solution.py:91
  112.9 1.8 copy.124
  114.7 1.4 convert_element_type.30
  116.1 1.8 copy.125
  117.9 0.8 convert_element_type.32
  118.7 1.0 compare_reduce_fusion
  119.7 1.0 fusion.8
  120.7 0.1 convolution_convert_fusion.2
  120.8 3.1 %convolution_convert_fusion = bf16[16,8,36,512]{3,2,1,0:T(8,128)(2,1)S(1)} fusion(bf16[16,132,512]{2,1,0:T(8,128)(2,1)} %bitcast.48, bf16[16,8,128]{2,1,0:T(8,128)(2,1)S(1)} %bitcast.56, s32[16,8,128]{2,1,0:T(8,128)S(1)} %convolution_convert_fusion.2, pred[16,8,128]{2,1,0:T(8,128)(4,1)S(1)} %bitcast.52), kind=kOutput, calls=%fused_computation.6 | convolution fusion | flops 608108544 | bytes 6930432 | tf_op jit(solution)/shard_map/blct,btd->blcd/dot_general | solution.py:111
  123.9 1.9 copy.115
  125.9 3.8 %copy.117.s_ref = bf16[8,576,512]{2,1,0:T(8,128)(2,1)} copy(bf16[8,576,512]{2,0,1:T(8,128)(2,1)S(1)} %bitcast.45) | data formatting | bytes 9437184 | tf_op jit(solution)/shard_map/reshape | solution.py:122
  129.7 1.5 convolution_convert_fusion.1
  131.2 1.9 copy.116
  133.1 4.0 %copy.118.g_ref = bf16[8,576,512]{2,1,0:T(8,128)(2,1)} copy(bf16[8,576,512]{2,0,1:T(8,128)(2,1)S(1)} %bitcast.46) | data formatting | bytes 9437184 | tf_op jit(solution)/shard_map/reshape | solution.py:123
  137.1 5.5 %pad_maximum_fusion = bf16[8,4,4,36,768]{4,0,3,2,1:T(8,128)(2,1)} fusion(bf16[8,2,4,36,768]{4,0,3,2,1:T(8,128)(2,1)} %collective-permute-done.1, bf16[8,1,4,36,768]{4,0,3,2,1:T(8,128)(2,1)S(1)} %collective-permute-done, bf16[8,1,4,36,768]{4,0,3,2,1:T(8,128)(2,1)S(1)} %copy.106), kind=kLoop, calls=%fused_computation.2 | loop fusion | flops 7077888 | bytes 14155776 | tf_op jit(solution)/shard_map/concatenate | solution.py:117
  142.6 6.9 %gather_fusion.1 = bf16[4,8,4,36,768]{4,1,3,2,0:T(8,128)(2,1)} fusion(bf16[8,4,4,36,768]{4,0,3,2,1:T(8,128)(2,1)} %pad_maximum_fusion, s32[1024]{0:T(1024)S(1)} %pad_clamp_fusion), kind=kCustom, calls=%fused_computation.1 | custom fusion | bytes 14155792 | tf_op jit(solution)/shard_map/jit(_take)/gather | solution.py:119
  149.5 8.7 %copy_select_fusion.h_ref = bf16[8,576,768]{2,1,0:T(8,128)(2,1)} fusion(bf16[8,576,768]{2,0,1:T(8,128)(2,1)} %bitcast.42, pred[576]{0:T(1024)(128)(4,1)S(1)} %broadcast_in_dim.100), kind=kLoop, calls=%fused_computation.3 | loop fusion | flops 3538944 | bytes 14156352 | tf_op jit(solution)/shard_map/jit(_take)/select_n | solution.py:119
  158.3 15.8 %shard_map.77 = (f32[8,768,512]{2,1,0:T(8,128)}, f32[8,576,1]{2,1,0:T(8,128)}) custom-call(bf16[8,576,768]{2,1,0:T(8,128)(2,1)} %copy_select_fusion.h_ref, bf16[8,576,512]{2,1,0:T(8,128)(2,1)} %copy.117.s_ref, bf16[8,576,512]{2,1,0:T(8,128)(2,1)} %copy.118.g_ref, bf16[8,768,512]{2,1,0:T(8,128)(2,1)} %w_ref.1), custom_call_target="tpu_custom_call" | custom-call | tf_op jit(solution)/shard_map/pallas_call | solution.py:36
  174.1 2.4 %reduce = f32[8,576]{1,0:T(8,128)S(1)} reduce(f32[8,576,1]{2,1,0:T(8,128)} %get-tuple-element.5, f32[]{:T(128)} %constant.36), dimensions={2}, to_apply=%get-tuple-element.5.reduce_sub_computation | reduce | bytes 36868 | tf_op jit(solution)/shard_map/pallas_call | solution.py:36
  176.5 0.1 reshape.95
  176.6 0.7 reshape.119
  177.3 3.5 %all-to-all-start.1 = ((f32[16,1,288]{2,1,0:T(1,128)}), f32[16,1,288]{2,1,0:T(1,128)S(1)}, u32[]{:S(2)}, u32[]{:S(2)}) async-start(f32[16,1,288]{2,1,0:T(1,128)} %reshape.119), calls=%async_computation.1 | async-start | bytes 49152 | tf_op jit(solution)/shard_map/all_to_all | solution.py:127
  180.9 6.5 %all-to-all-done.1 = f32[16,1,288]{2,1,0:T(1,128)S(1)} async-done(((f32[16,1,288]{2,1,0:T(1,128)}), f32[16,1,288]{2,1,0:T(1,128)S(1)}, u32[]{:S(2)}, u32[]{:S(2)}) %all-to-all-start.1) | async-done | bytes 18464 | tf_op jit(solution)/shard_map/all_to_all | solution.py:127
  187.4 0.5 broadcast.102
  188.0 0.7 reduce.1
  188.8 0.1 copy.120
  188.9 0.8 select_reduce_fusion
  189.7 0.6 select_reduce_fusion.1
  (30 shorter events, 0.3 us)
Async XLA Ops:
  7.2 5.1 %copy-start.3 = (s32[128,8]{0,1:T(8,128)S(1)}, s32[128,8]{0,1:T(8,128)}, u32[]{:S(2)}) copy-start(s32[128,8]{0,1:T(8,128)} %param.8) | copy-start | bytes 12292
  7.2 5.1 %copy-start.5 = (bf16[128,8]{0,1:T(8,128)(2,1)S(1)}, bf16[128,8]{0,1:T(8,128)(2,1)}, u32[]{:S(2)}) copy-start(bf16[128,8]{0,1:T(8,128)(2,1)} %param.7) | copy-start | bytes 6148
  7.2 99.7 %all-gather.3.cloned.1.call-start = ((), (), s32[]{:S(2)}) async-start(), calls=%async_computation.2 | async-start | bytes 2785280 | tf_op jit(solution)/shard_map/all_gather | solution.py:86
  9.2 47.7 %collective-permute-start = (bf16[8,1,4,36,768]{4,0,3,2,1:T(8,128)(2,1)S(1)}, bf16[8,1,4,36,768]{4,0,3,2,1:T(8,128)(2,1)S(1)}, u32[]{:S(2)}, u32[]{:S(2)}) collective-permute-start(bf16[8,1,4,36,768]{4,0,3,2,1:T(8,128)(2,1)S(1)} %copy.106), channel_id=1, source_target_pairs={{0,2},{1,3},{2,0},{3,1},{4,6},{5,7},{6,4},{7,5},{8,10},{9,11},{10,... | collective-permute-start | bytes 5308424 | tf_op jit(solution)/shard_map/ppermute | solution.py:71
  56.9 2.1 %copy-start = (s32[4]{0:T(128)S(1)}, s32[4]{0:T(128)}, u32[]{:S(2)}) copy-start(s32[4]{0:T(128)} %constant.34.clone) | copy-start | bytes 52
  59.1 78.0 %collective-permute-start.1 = (bf16[8,2,4,36,768]{4,0,3,2,1:T(8,128)(2,1)}, bf16[8,2,4,36,768]{4,0,3,2,1:T(8,128)(2,1)}, u32[]{:S(2)}, u32[]{:S(2)}) collective-permute-start(bf16[8,2,4,36,768]{4,0,3,2,1:T(8,128)(2,1)} %pad_maximum_fusion.1), channel_id=1, source_target_pairs={{0,1},{1,0},{2,3},{3,2},{4,5},{5,4},{6,7},{7,6},{8,9},{9,8},{10,11... | collective-permute-start | bytes 10616840 | tf_op jit(solution)/shard_map/ppermute | solution.py:72
  59.7 0.5 copy-start.6
  125.9 3.8 %copy-start.1 = (bf16[16,132,1,512]{3,1,2,0:T(8,128)(2,1)S(1)}, bf16[16,132,1,512]{3,1,2,0:T(8,128)(2,1)}, u32[]{:S(2)}) copy-start(bf16[16,132,1,512]{3,1,2,0:T(8,128)(2,1)} %all-gather.3.cloned.1.call-done) | copy-start | bytes 6488068
  158.3 22.6 %copy-start.4 = (s32[128,32]{0,1:T(8,128)S(1)}, s32[128,32]{0,1:T(8,128)}, u32[]{:S(2)}) copy-start(s32[128,32]{0,1:T(8,128)} %convolution_convert_fusion.3) | copy-start | bytes 49156
  158.3 30.6 %copy-start.2 = (pred[128,8,32]{0,2,1:T(8,128)(4,1)S(1)}, pred[128,8,32]{0,2,1:T(8,128)(4,1)}, u32[]{:S(2)}) copy-start(pred[128,8,32]{0,2,1:T(8,128)(4,1)} %get-tuple-element.9) | copy-start | bytes 98308
  177.3 10.1 %all-to-all-start.1 = ((f32[16,1,288]{2,1,0:T(1,128)}), f32[16,1,288]{2,1,0:T(1,128)S(1)}, u32[]{:S(2)}, u32[]{:S(2)}) async-start(f32[16,1,288]{2,1,0:T(1,128)} %reshape.119), calls=%async_computation.1 | async-start | bytes 49152 | tf_op jit(solution)/shard_map/all_to_all | solution.py:127
Sparse Core Ops, SparseCore 0:
  57.1 49.8 all-gather.2

commit v4 on v3

--- a/solution.py
+++ b/solution.py
@@ -7,9 +7,13 @@
 
 def expert_body(h_ref, s_ref, g_ref, w_ref, wg_ref, slot_ref):
     chunk = pl.program_id(1)
-    h = h_ref[0]
+    blocks, slots, hidden_width = h_ref.shape[1:]
+    col_width = s_ref.shape[3]
+    rows = blocks * slots
+    h = h_ref[0].reshape(rows, hidden_width)
     part = lax.dot_general(
-        h, s_ref[0], (((0,), (0,)), ((), ())), preferred_element_type=jnp.float32
+        h, s_ref[:, 0].reshape(rows, col_width), (((0,), (0,)), ((), ())),
+        preferred_element_type=jnp.float32,
     )
 
     @pl.when(chunk == 0)
@@ -21,34 +25,36 @@
         wg_ref[0] = wg_ref[0] + part
 
     out = jnp.dot(h, w_ref[0], preferred_element_type=jnp.float32)
-    slot_ref[0] = jnp.sum(g_ref[0].astype(jnp.float32) * out, axis=1, keepdims=True)
+    g = g_ref[:, 0].reshape(rows, col_width).astype(jnp.float32)
+    slot_ref[0] = jnp.sum(g * out, axis=1, keepdims=True)
 
 
 def expert_kernel(hidden_rows, scaled_rows, grad_rows, weight):
-    local_count, slot_rows, hidden_width = hidden_rows.shape
-    col_width = scaled_rows.shape[2]
-    chunk = slot_rows
-    for size in (576, 512, 384, 256, 128):
-        if slot_rows % size == 0:
+    local_count, block_count, slots, hidden_width = hidden_rows.shape
+    col_width = scaled_rows.shape[3]
+    chunk = block_count
+    for size in (16, 8, 4, 2, 1):
+        if block_count % size == 0:
             chunk = size
             break
-    steps = slot_rows // chunk
+    steps = block_count // chunk
+    rows = chunk * slots
     return pl.pallas_call(
         expert_body,
         grid=(local_count, steps),
         in_specs=[
-            pl.BlockSpec((1, chunk, hidden_width), lambda l, r: (l, r, 0)),
-            pl.BlockSpec((1, chunk, col_width), lambda l, r: (l, r, 0)),
-            pl.BlockSpec((1, chunk, col_width), lambda l, r: (l, r, 0)),
+            pl.BlockSpec((1, chunk, slots, hidden_width), lambda l, r: (l, r, 0, 0)),
+            pl.BlockSpec((chunk, 1, slots, col_width), lambda l, r: (r, l, 0, 0)),
+            pl.BlockSpec((chunk, 1, slots, col_width), lambda l, r: (r, l, 0, 0)),
             pl.BlockSpec((1, hidden_width, col_width), lambda l, r: (l, 0, 0)),
         ],
         out_specs=[
             pl.BlockSpec((1, hidden_width, col_width), lambda l, r: (l, 0, 0)),
-            pl.BlockSpec((1, chunk, 1), lambda l, r: (l, r, 0)),
+            pl.BlockSpec((1, rows, 1), lambda l, r: (l, r, 0)),
         ],
         out_shape=[
             jax.ShapeDtypeStruct((local_count, hidden_width, col_width), jnp.float32),
-            jax.ShapeDtypeStruct((local_count, slot_rows, 1), jnp.float32),
+            jax.ShapeDtypeStruct((local_count, block_count * slots, 1), jnp.float32),
         ],
     )(hidden_rows, scaled_rows, grad_rows, weight)
 
@@ -68,13 +74,6 @@
     bf16 = jnp.bfloat16
     my_dp = lax.axis_index("dp")
 
-    fetched = lax.ppermute(hidden, "dp", [(j, j ^ 2) for j in range(shards)])
-    paired = lax.ppermute(
-        jnp.concatenate([hidden, fetched], axis=1), "dp", [(j, j ^ 1) for j in range(shards)]
-    )
-    pieces = [hidden, fetched, paired[:, 0:1], paired[:, 1:2]]
-    piece_replica = [my_dp, my_dp ^ 2, my_dp ^ 1, my_dp ^ 3]
-
     meta = jnp.concatenate([expert_ids.astype(bf16), gate_weights], axis=1).reshape(-1)
     meta_len = meta.shape[0]
     meta_rows = -(-meta_len // col_width)
@@ -83,6 +82,12 @@
     cols = jnp.concatenate([cols, jnp.broadcast_to(meta, (meta_rows, shards, col_width))], axis=0)
     cols = lax.all_to_all(cols, "dp", split_axis=1, concat_axis=0, tiled=True)
     cols = cols.reshape(shards, tok_rows + meta_rows, col_width)
+
+    hidden_sent, cols = lax.optimization_barrier((hidden, cols))
+    fetched = lax.ppermute(hidden_sent, "dp", [(j, j ^ 2) for j in range(shards)])
+    paired = lax.ppermute(
+        jnp.concatenate([hidden_sent, fetched], axis=1), "dp", [(j, j ^ 1) for j in range(shards)]
+    )
     got = lax.all_gather(cols, "expert", axis=0, tiled=False)
     got = got.reshape(block_count, tok_rows + meta_rows, col_width)
     grad_all = got[:, :tok_rows]
@@ -99,7 +104,8 @@
     rank = jnp.einsum(
         "bul,ut->btl", chose.astype(bf16), before, preferred_element_type=f32
     ).astype(jnp.int32)
-    slot_ids = jnp.arange(capacity, dtype=jnp.int32)
+    padded = -(-capacity // 8) * 8
+    slot_ids = jnp.arange(padded, dtype=jnp.int32)
     chose_t = chose.transpose(0, 2, 1)
     rank_t = rank.transpose(0, 2, 1)
     gate_t = gate_hit.transpose(0, 2, 1)
@@ -111,18 +117,18 @@
     scaled = jnp.einsum(
         "blct,btd->blcd", select_gate, grad_all, preferred_element_type=f32
     ).astype(bf16)
-    grad_rows = grad_rows.reshape(peer_count, shards, local_count, capacity, col_width)
-    scaled = scaled.reshape(peer_count, shards, local_count, capacity, col_width)
 
-    hidden_all = jnp.concatenate([hidden, fetched, paired], axis=1)
-    piece_of = jnp.array([0, 2, 1, 3], jnp.int32)[jnp.arange(shards, dtype=jnp.int32) ^ my_dp]
-    hidden_all = jnp.take(hidden_all, piece_of, axis=1)
-    slot_rows = shards * peer_count * capacity
-    hidden_rows = hidden_all.reshape(local_count, slot_rows, hidden_width)
-    scaled_rows = scaled.transpose(2, 1, 0, 3, 4).reshape(local_count, slot_rows, col_width)
-    grad_slot_rows = grad_rows.transpose(2, 1, 0, 3, 4).reshape(local_count, slot_rows, col_width)
-    weight_grad, slot_part = expert_kernel(hidden_rows, scaled_rows, grad_slot_rows, down_weight)
-    slot_part = slot_part.reshape(local_count, shards, peer_count, capacity).transpose(2, 1, 0, 3)
+    offset = jnp.arange(shards, dtype=jnp.int32) ^ my_dp
+    own, far, near, near_far = hidden, fetched, paired[:, 0:1], paired[:, 1:2]
+    off = offset[None, :, None, None, None]
+    hidden_all = jnp.where(
+        off == 0, own, jnp.where(off == 2, far, jnp.where(off == 1, near, near_far))
+    )
+    hidden_all = hidden_all.transpose(0, 2, 1, 3, 4).reshape(local_count, block_count, capacity, hidden_width)
+    hidden_all = jnp.pad(hidden_all, ((0, 0), (0, 0), (0, padded - capacity), (0, 0)))
+    weight_grad, slot_part = expert_kernel(hidden_all, scaled, grad_rows, down_weight)
+    slot_part = slot_part.reshape(local_count, block_count, padded)[:, :, :capacity]
+    slot_part = slot_part.transpose(1, 0, 2)
     send_back = slot_part.reshape(block_count, local_count, capacity)
     returned = lax.all_to_all(
         send_back, ("expert", "dp"), split_axis=0, concat_axis=0, tiled=True
@@ -138,7 +144,7 @@
     own_slot = jnp.sum(jnp.where(own_hit, own_rank[:, None, :], 0), axis=2)
     by_slot = jnp.sum(jnp.where(own_hit[:, :, :, None], slot_grad[None, None], 0.0), axis=2)
     gate_grad = jnp.sum(
-        jnp.where(own_slot[:, :, None] == slot_ids[None, None, :], by_slot, 0.0), axis=2
+        jnp.where(own_slot[:, :, None] == slot_ids[None, None, :capacity], by_slot, 0.0), axis=2
     )
     return (weight_grad, gate_grad)
 

time: 198 us -> 161 us (0.81)
  blocking collectives: 34.9 us -> 13.3 us
  other arithmetic: 28.5 us -> 20.5 us
  local copies, waits for them, and re-layouts: 40.4 us -> 33 us
  waiting for transfers between devices: 51.2 us -> 47.2 us
  matrix products: 5.52 us -> 8.49 us
  Pallas kernels: 15.8 us -> 18.1 us
    all_gather x1, waiting for transfers between devices: 44.6 us -> 0.59 us  [per_device(): got = lax.all_gather(cols, 'expert', axis=0, tiled=False)]
    ppermute x2, waiting for transfers between devices: 0.01 us -> 40.1 us  [the longest x1 40.1 us: per_device(): lax.ppermute(hidden_sent, 'dp', [(j, j ^ 2) for j in range(shards)])]
    all_to_all x1, blocking collectives: 34.9 us -> 13.3 us  [per_device(): cols = lax.all_to_all(cols, 'dp', split_axis=1, concat_axis=0, tiled=True)]
    broadcast_in_dim x2 -> x15, local copies, waits for them, and re-layouts: 0.18 us -> 19.3 us  [the longest x7 11.1 us: per_device(): jnp.where(off == 1, near, near_far)]
    reshape x5 -> x1, local copies, waits for them, and re-layouts: 11.8 us -> 0.09 us  [per_device(): slot_part.reshape(local_count, block_count, padded)[:, :, :capacity]]
    gather x2 -> x0, local copies, waits for them, and re-layouts: 7.59 us -> none  [the longest x1 6.95 us: per_device(): hidden_all = jnp.take(hidden_all, piece_of, axis=1)]
    pad x0 -> x1, local copies, waits for them, and re-layouts: none -> 3.79 us  [per_device(): jnp.pad(hidden_all, ((0, 0), (0, 0), (0, padded - capacity), (0, 0)))]
    concatenate x2 -> x1, other arithmetic: 7.58 us -> 4.28 us  [per_device(): jnp.concatenate([hidden_sent, fetched], axis=1)]
  transfers between devices with their start and end apart: 4 -> 4, of which waited for: 2 -> 3; matrix products, arithmetic and copies ran while one was open for 23% -> 13% of each run, Pallas kernels for 0% -> 0%
where the time goes in v4:
time: 161 us; the launch traced here: 160 us
  waiting for transfers between devices  47.2 us (29%)
  local copies, waits for them, and re-layouts  33 us (20%)
  other arithmetic  20.5 us (13%)
  Pallas kernels  18.1 us (11%)
  between operations  14.3 us (9%)
  blocking collectives  13.3 us (8%)
  matrix products  8.49 us (5%)
  starting transfers between devices  5.34 us (3%)
    ppermute x1, waiting for transfers between devices, per_device(): lax.ppermute(hidden_sent, 'dp', [(j, j ^ 2) for j in range(shards)])  40.1 us
    pallas_call x1, Pallas kernels, expert_kernel(): pl.pallas_call(expert_body, grid=(local_count, steps), in_specs=[pl.Block...  18.1 us
    all_to_all x1, blocking collectives, per_device(): cols = lax.all_to_all(cols, 'dp', split_axis=1, concat_axis=0, tiled=True)  13.3 us
    broadcast_in_dim x7, local copies, waits for them, and re-layouts, per_device(): jnp.where(off == 1, near, near_far)  11.1 us
    select_n x1, other arithmetic, per_device(): jnp.where(off == 0, own, jnp.where(off == 2, far, jnp.where(off == 1, nea...  8.88 us
    all_to_all x1, waiting for transfers between devices, per_device(): lax.all_to_all(send_back, ('expert', 'dp'), split_axis=0, concat_axis=0,...  6.52 us
    unnamed x21, local copies, waits for them, and re-layouts  5.81 us
    broadcast_in_dim x4, local copies, waits for them, and re-layouts, per_device(): jnp.where(off == 2, far, jnp.where(off == 1, near, near_far))  5.45 us
  transfers between devices with their start and end apart: 4, of which 3 were waited for; matrix products, arithmetic and copies ran while one was open for 13% of the time, Pallas kernels for 0%

profile of v4, /device:TPU:0, one launch (start us, length us, event | category | flops | bytes accessed | tf_op | source)
XLA Modules:
  0.0 160.2 jit_solution(13754813698074429078)
XLA Ops:
  7.2 0.7 convert_element_type.31
  7.9 0.7 pad_maximum_fusion.2
  8.6 0.1 copy.77
  8.7 0.1 broadcast_in_dim.172
  8.8 0.2 copy.78
  9.0 1.3 copy.76
  10.4 0.2 pad_maximum_fusion.1
  10.6 0.5 copy.79
  11.1 13.3 %all_to_all.20 = bf16[132,4,512]{2,0,1:T(8,128)(2,1)} all-to-all(bf16[132,4,512]{2,0,1:T(8,128)(2,1)S(1)} %copy.79), channel_id=1, replica_groups=mesh['groups'=2,'expert'=4,'dp'=4] {'dp'}, dimensions={1} | all-to-all | bytes 1081344 | tf_op jit(solution)/shard_map/all_to_all | solution.py:83
  24.4 0.4 collective-permute-start
  24.8 40.1 %collective-permute-done = bf16[8,1,4,36,768]{4,2,3,1,0:T(4,128)(2,1)S(1)} collective-permute-done((bf16[8,1,4,36,768]{4,2,3,1,0:T(4,128)(2,1)S(1)}, bf16[8,1,4,36,768]{4,2,3,1,0:T(4,128)(2,1)S(1)}, u32[]{:S(2)}, u32[]{:S(2)}) %collective-permute-start) | collective-permute-done | bytes 1769504 | tf_op jit(solution)/shard_map/ppermute | solution.py:87
  64.9 4.3 %pad_maximum_fusion = bf16[8,2,4,36,768]{4,2,3,1,0:T(4,128)(2,1)} fusion(bf16[8,1,4,36,768]{4,2,3,1,0:T(4,128)(2,1)S(1)} %collective-permute-done, bf16[8,1,4,36,768]{4,2,3,1,0:T(4,128)(2,1)S(1)} %copy-done.3), kind=kLoop, calls=%fused_computation.2 | loop fusion | flops 1769472 | bytes 7077888 | tf_op jit(solution)/shard_map/concatenate | solution.py:89
  69.2 1.6 copy.75
  71.0 0.6 broadcast_in_dim.164
  71.6 0.6 fusion.9
  72.2 0.7 convolution_convert_fusion.3
  72.9 1.6 %copy.80 = bf16[8,4,36,768]{3,2,1,0:T(8,128)(2,1)} copy(bf16[8,4,36,768]{3,1,2,0:T(4,128)(2,1)S(1)} %bitcast.40) | data formatting | bytes 3538944 | tf_op jit(solution)/shard_map/jit(_where)/broadcast_in_dim | solution.py:125
  74.6 0.6 all-gather.3.cloned.1.call-done
  75.2 1.1 slice.34
  76.2 0.4 reshape_reshape.3
  76.6 1.0 fusion.16
  77.6 1.2 copy.94
  78.9 0.2 copy.93
  79.1 0.1 compare_reduce_fusion
  79.2 0.1 fusion.8
  79.4 0.1 convolution_convert_fusion.2
  79.5 3.8 %convolution_convert_fusion.1.g_ref = bf16[16,8,40,512]{3,2,1,0:T(8,128)(2,1)} fusion(bf16[16,132,512]{2,1,0:T(8,128)(2,1)S(1)} %copy-done, s32[16,8,128]{2,1,0:T(8,128)S(1)} %convolution_convert_fusion.2, pred[16,8,128]{2,1,0:T(8,128)(4,1)S(1)} %bitcast.43), kind=kOutput, calls=%fused_computation.4 | convolution fusion | flops 675020800 | bytes 7421952 | tf_op jit(solution)/shard_map/blct,btd->blcd/dot_general | solution.py:114
  83.4 3.8 %convolution_convert_fusion.s_ref = bf16[16,8,40,512]{3,2,1,0:T(8,128)(2,1)} fusion(bf16[16,132,512]{2,1,0:T(8,128)(2,1)S(1)} %copy-done, bf16[16,8,128]{2,1,0:T(8,128)(2,1)S(1)} %bitcast.45, s32[16,8,128]{2,1,0:T(8,128)S(1)} %convolution_convert_fusion.2, pred[16,8,128]{2,1,0:T(8,128)(4,1)S(1)} %bitcast.44), kind=kOutput, calls=%fused_computation.3 | convolution fusion | flops 675676160 | bytes 7454720 | tf_op jit(solution)/shard_map/blct,btd->blcd/dot_general | solution.py:117
  87.1 3.2 %slice_bitcast_fusion.1 = (bf16[8,4,36,768]{3,1,2,0:T(4,128)(2,1)S(1)}, bf16[8,4,36,768]{3,1,2,0:T(4,128)(2,1)S(1)}) fusion(bf16[8,2,4,36,768]{4,2,3,1,0:T(4,128)(2,1)} %collective-permute-done.1), kind=kLoop, calls=%fused_computation.9 | loop fusion | bytes 7077888 | tf_op jit(solution)/shard_map/jit(_where)/broadcast_in_dim | solution.py:125
  90.4 0.3 copy.81
  90.6 0.3 copy.82
  90.9 1.3 copy-done.1
  92.2 0.5 broadcast_in_dim.167
  92.7 1.0 copy-done.2
  93.7 3.7 %broadcast_in_dim.175 = bf16[8,4,4,36,768]{4,3,2,1,0:T(8,128)(2,1)} broadcast(bf16[8,4,36,768]{3,2,1,0:T(8,128)(2,1)S(1)} %copy-done.2), dimensions={0,1,3,4} | broadcast | bytes 8847360 | tf_op jit(solution)/shard_map/jit(_where)/broadcast_in_dim | solution.py:125
  97.5 3.6 %broadcast_in_dim.181 = bf16[8,4,4,36,768]{4,3,2,1,0:T(8,128)(2,1)} broadcast(bf16[8,4,36,768]{3,2,1,0:T(8,128)(2,1)S(1)} %copy.81), dimensions={0,1,3,4} | broadcast | bytes 8847360 | tf_op jit(solution)/shard_map/jit(_where)/broadcast_in_dim | solution.py:125
  101.0 3.7 %broadcast_in_dim.184 = bf16[8,4,4,36,768]{4,3,2,1,0:T(8,128)(2,1)} broadcast(bf16[8,4,36,768]{3,2,1,0:T(8,128)(2,1)S(1)} %copy.82), dimensions={0,1,3,4} | broadcast | bytes 8847360 | tf_op jit(solution)/shard_map/jit(_where)/broadcast_in_dim | solution.py:125
  104.7 8.9 %select_select_fusion = bf16[8,16,36,768]{3,2,1,0:T(8,128)(2,1)S(1)} fusion(bf16[8,16,36,768]{3,2,1,0:T(8,128)(2,1)S(1)} %bitcast.35, bf16[8,16,36,768]{3,2,1,0:T(8,128)(2,1)} %bitcast.36, bf16[8,16,36,768]{3,2,1,0:T(8,128)(2,1)} %bitcast.37, bf16[8,16,36,768]{3,2,1,0:T(8,128)(2,1)} %bitcast.38, pred[16]{0:T(512)(128)(4,1)S(1)} %broadcast_in_dim.178, ...), kind=kLoop, calls=%fused_computation | loop fusion | flops 10616832 | bytes 35389488 | tf_op jit(solution)/shard_map/jit(_where)/select_n | solution.py:124
  113.6 3.8 %pad.4.h_ref = bf16[8,16,40,768]{3,2,1,0:T(8,128)(2,1)} pad(bf16[8,16,36,768]{3,2,1,0:T(8,128)(2,1)S(1)} %select_select_fusion, bf16[]{:T(256)} %constant.8.clone.1), padding=0_0x0_0x0_4x0_0 | pad | bytes 14942210 | tf_op jit(solution)/shard_map/jit(_pad)/pad | solution.py:128
  117.4 18.1 %shard_map.68 = (f32[8,768,512]{2,1,0:T(8,128)}, f32[8,640,1]{2,1,0:T(8,128)}) custom-call(bf16[8,16,40,768]{3,2,1,0:T(8,128)(2,1)} %pad.4.h_ref, bf16[16,8,40,512]{3,2,1,0:T(8,128)(2,1)} %convolution_convert_fusion.s_ref, bf16[16,8,40,512]{3,2,1,0:T(8,128)(2,1)} %convolution_convert_fusion.1.g_ref, bf16[8,768,512]{2,1,0:T(8,128)(2,1)} %w_ref.1), custom_call_target="tpu_custom_call" | custom-call | tf_op jit(solution)/shard_map/pallas_call | solution.py:42
  135.5 2.5 %reduce = f32[8,640]{1,0:T(8,128)S(1)} reduce(f32[8,640,1]{2,1,0:T(8,128)} %get-tuple-element.9, f32[]{:T(128)} %constant.25), dimensions={2}, to_apply=%get-tuple-element.9.reduce_sub_computation | reduce | bytes 40964 | tf_op jit(solution)/shard_map/pallas_call | solution.py:42
  138.1 0.7 reshape.73
  138.8 4.9 %all-to-all-start.1 = ((f32[16,1,288]{2,1,0:T(1,128)}), f32[16,1,288]{2,1,0:T(1,128)S(1)}, u32[]{:S(2)}, u32[]{:S(2)}) async-start(f32[16,1,288]{2,1,0:T(1,128)} %reshape.73), calls=%async_computation.1 | async-start | bytes 49152 | tf_op jit(solution)/shard_map/all_to_all | solution.py:133
  143.8 6.5 %all-to-all-done.1 = f32[16,1,288]{2,1,0:T(1,128)S(1)} async-done(((f32[16,1,288]{2,1,0:T(1,128)}), f32[16,1,288]{2,1,0:T(1,128)S(1)}, u32[]{:S(2)}, u32[]{:S(2)}) %all-to-all-start.1) | async-done | bytes 18464 | tf_op jit(solution)/shard_map/all_to_all | solution.py:133
  150.4 0.5 broadcast.78
  150.9 0.7 reduce.1
  151.8 0.8 select_reduce_fusion
  152.6 0.7 select_reduce_fusion.1
  (37 shorter events, 0.7 us)
Async XLA Ops:
  7.2 68.0 %all-gather.3.cloned.1.call-start = ((), (), s32[]{:S(2)}) async-start(), calls=%async_computation.2 | async-start | bytes 2785280 | tf_op jit(solution)/shard_map/all_gather | solution.py:91
  10.3 14.1 %copy-start.3 = (bf16[8,1,4,36,768]{4,2,3,1,0:T(4,128)(2,1)S(1)}, bf16[8,1,4,36,768]{4,2,3,1,0:T(4,128)(2,1)}, u32[]{:S(2)}) copy-start(bf16[8,1,4,36,768]{4,2,3,1,0:T(4,128)(2,1)} %param.8) | copy-start | bytes 5308420
  24.4 40.5 %collective-permute-start = (bf16[8,1,4,36,768]{4,2,3,1,0:T(4,128)(2,1)S(1)}, bf16[8,1,4,36,768]{4,2,3,1,0:T(4,128)(2,1)S(1)}, u32[]{:S(2)}, u32[]{:S(2)}) collective-permute-start(bf16[8,1,4,36,768]{4,2,3,1,0:T(4,128)(2,1)S(1)} %copy-done.3), channel_id=1, source_target_pairs={{0,2},{1,3},{2,0},{3,1},{4,6},{5,7},{6,4},{7,5},{8,10},{9,11},{10,... | collective-permute-start | bytes 5308424 | tf_op jit(solution)/shard_map/ppermute | solution.py:87
  69.2 2.4 %copy-start.5 = (s32[128,8]{0,1:T(8,128)S(1)}, s32[128,8]{0,1:T(8,128)}, u32[]{:S(2)}) copy-start(s32[128,8]{0,1:T(8,128)} %param.7) | copy-start | bytes 12292
  69.2 18.0 %collective-permute-start.1 = (bf16[8,2,4,36,768]{4,2,3,1,0:T(4,128)(2,1)}, bf16[8,2,4,36,768]{4,2,3,1,0:T(4,128)(2,1)}, u32[]{:S(2)}, u32[]{:S(2)}) collective-permute-start(bf16[8,2,4,36,768]{4,2,3,1,0:T(4,128)(2,1)} %pad_maximum_fusion), channel_id=1, source_target_pairs={{0,1},{1,0},{2,3},{3,2},{4,5},{5,4},{6,7},{7,6},{8,9},{9,8},{10,11... | collective-permute-start | bytes 10616840 | tf_op jit(solution)/shard_map/ppermute | solution.py:88
  75.2 4.4 %copy-start = (bf16[16,132,512]{2,1,0:T(8,128)(2,1)S(1)}, bf16[16,132,512]{2,1,0:T(8,128)(2,1)}, u32[]{:S(2)}) copy-start(bf16[16,132,512]{2,1,0:T(8,128)(2,1)} %all-gather.3.cloned.1.call-done) | copy-start | bytes 6488068
  90.6 1.5 copy-start.1
  92.2 1.5 copy-start.2
  101.0 3.7 %copy-start.7 = (pred[16]{0:T(512)(128)(4,1)S(1)}, pred[16]{0:T(512)(128)(4,1)}, u32[]{:S(2)}) copy-start(pred[16]{0:T(512)(128)(4,1)} %broadcast_in_dim.164) | copy-start | bytes 52
  135.5 8.3 %copy-start.6 = (s32[128,32]{0,1:T(8,128)S(1)}, s32[128,32]{0,1:T(8,128)}, u32[]{:S(2)}) copy-start(s32[128,32]{0,1:T(8,128)} %convolution_convert_fusion.3) | copy-start | bytes 49156
  135.5 16.3 %copy-start.4 = (pred[128,8,32]{0,2,1:T(8,128)(4,1)S(1)}, pred[128,8,32]{0,2,1:T(8,128)(4,1)}, u32[]{:S(2)}) copy-start(pred[128,8,32]{0,2,1:T(8,128)(4,1)} %get-tuple-element.15) | copy-start | bytes 98308
  138.8 11.5 %all-to-all-start.1 = ((f32[16,1,288]{2,1,0:T(1,128)}), f32[16,1,288]{2,1,0:T(1,128)S(1)}, u32[]{:S(2)}, u32[]{:S(2)}) async-start(f32[16,1,288]{2,1,0:T(1,128)} %reshape.73), calls=%async_computation.1 | async-start | bytes 49152 | tf_op jit(solution)/shard_map/all_to_all | solution.py:133
Sparse Core Ops, SparseCore 0:
  24.9 50.1 all-gather.2

commit v5 on v4

--- a/solution.py
+++ b/solution.py
@@ -82,12 +82,19 @@
     cols = jnp.concatenate([cols, jnp.broadcast_to(meta, (meta_rows, shards, col_width))], axis=0)
     cols = lax.all_to_all(cols, "dp", split_axis=1, concat_axis=0, tiled=True)
     cols = cols.reshape(shards, tok_rows + meta_rows, col_width)
+    piece_xor = jnp.array([0, 2, 1, 3], jnp.int32)
+    cols = jnp.take(cols, piece_xor ^ my_dp, axis=0)
 
     hidden_sent, cols = lax.optimization_barrier((hidden, cols))
-    fetched = lax.ppermute(hidden_sent, "dp", [(j, j ^ 2) for j in range(shards)])
-    paired = lax.ppermute(
-        jnp.concatenate([hidden_sent, fetched], axis=1), "dp", [(j, j ^ 1) for j in range(shards)]
-    )
+    halves = [hidden_sent[: local_count // 2], hidden_sent[local_count // 2 :]]
+    if local_count < 2:
+        halves = [hidden_sent]
+    near = [lax.ppermute(h, "dp", [(j, j ^ 1) for j in range(shards)]) for h in halves]
+    far = [lax.ppermute(h, "dp", [(j, j ^ 2) for j in range(shards)]) for h in halves]
+    near_far = [lax.ppermute(h, "dp", [(j, j ^ 1) for j in range(shards)]) for h in far]
+    near = jnp.concatenate(near, axis=0)
+    far = jnp.concatenate(far, axis=0)
+    near_far = jnp.concatenate(near_far, axis=0)
     got = lax.all_gather(cols, "expert", axis=0, tiled=False)
     got = got.reshape(block_count, tok_rows + meta_rows, col_width)
     grad_all = got[:, :tok_rows]
@@ -118,17 +125,14 @@
         "blct,btd->blcd", select_gate, grad_all, preferred_element_type=f32
     ).astype(bf16)
 
-    offset = jnp.arange(shards, dtype=jnp.int32) ^ my_dp
-    own, far, near, near_far = hidden, fetched, paired[:, 0:1], paired[:, 1:2]
-    off = offset[None, :, None, None, None]
-    hidden_all = jnp.where(
-        off == 0, own, jnp.where(off == 2, far, jnp.where(off == 1, near, near_far))
-    )
+    hidden_all = jnp.concatenate([hidden, far, near, near_far], axis=1)
     hidden_all = hidden_all.transpose(0, 2, 1, 3, 4).reshape(local_count, block_count, capacity, hidden_width)
     hidden_all = jnp.pad(hidden_all, ((0, 0), (0, 0), (0, padded - capacity), (0, 0)))
     weight_grad, slot_part = expert_kernel(hidden_all, scaled, grad_rows, down_weight)
     slot_part = slot_part.reshape(local_count, block_count, padded)[:, :, :capacity]
-    slot_part = slot_part.transpose(1, 0, 2)
+    slot_part = slot_part.transpose(1, 0, 2).reshape(peer_count, shards, local_count, capacity)
+    piece_of = jnp.array([0, 2, 1, 3], jnp.int32)[jnp.arange(shards, dtype=jnp.int32) ^ my_dp]
+    slot_part = jnp.take(slot_part, piece_of, axis=1)
     send_back = slot_part.reshape(block_count, local_count, capacity)
     returned = lax.all_to_all(
         send_back, ("expert", "dp"), split_axis=0, concat_axis=0, tiled=True

time: 161 us -> 173 us (1.075)
  waiting for transfers between devices: 47.2 us -> 83.4 us
  blocking collectives: 13.3 us -> 0 us
  local copies, waits for them, and re-layouts: 33 us -> 19.8 us
  starting transfers between devices: 5.34 us -> 10.3 us
  other arithmetic: 20.5 us -> 17.8 us
    all_gather x1, waiting for transfers between devices: 0.59 us -> 30.9 us  [per_device(): got = lax.all_gather(cols, 'expert', axis=0, tiled=False)]
    broadcast_in_dim x15 -> x2, local copies, waits for them, and re-layouts: 19.3 us -> 0.61 us  [per_device(): slot_part = jnp.take(slot_part, piece_of, axis=1)]
    all_to_all x1 -> x0, blocking collectives: 13.3 us -> none  [per_device(): cols = lax.all_to_all(cols, 'dp', split_axis=1, concat_axis=0, tiled=True)]
    all_to_all x0 -> x1, waiting for transfers between devices: none -> 8.52 us  [per_device(): cols = lax.all_to_all(cols, 'dp', split_axis=1, concat_axis=0, tiled=True)]
    transpose x0 -> x1, other arithmetic: none -> 8.17 us  [per_device(): hidden_all.transpose(0, 2, 1, 3, 4)]
    select_n x1 -> x4, other arithmetic: 8.88 us -> 1.01 us  [the longest x1 0.91 us: per_device(): cols = jnp.take(cols, piece_xor ^ my_dp, axis=0)]
    transpose x2 -> x3, local copies, waits for them, and re-layouts: 0.03 us -> 4.57 us  [the longest x1 4.53 us: per_device(): hidden_all.transpose(0, 2, 1, 3, 4)]
    concatenate x1 -> x0, other arithmetic: 4.28 us -> none  [per_device(): jnp.concatenate([hidden_sent, fetched], axis=1)]
  transfers between devices with their start and end apart: 4 -> 9, of which waited for: 3 -> 6; matrix products, arithmetic and copies ran while one was open for 13% -> 12% of each run, Pallas kernels for 0% -> 0%
where the time goes in v5:
time: 173 us; the launch traced here: 172 us
  waiting for transfers between devices  83.4 us (48%)
  local copies, waits for them, and re-layouts  19.8 us (11%)
  Pallas kernels  18.1 us (10%)
  other arithmetic  17.8 us (10%)
  between operations  14.3 us (8%)
  starting transfers between devices  10.3 us (6%)
  matrix products  8.5 us (5%)
    ppermute x2, waiting for transfers between devices, per_device(): lax.ppermute(h, 'dp', [(j, j ^ 2) for j in range(shards)])  36.3 us
    all_gather x1, waiting for transfers between devices, per_device(): got = lax.all_gather(cols, 'expert', axis=0, tiled=False)  30.9 us
    pallas_call x1, Pallas kernels, expert_kernel(): pl.pallas_call(expert_body, grid=(local_count, steps), in_specs=[pl.Block...  18.1 us
    all_to_all x1, waiting for transfers between devices, per_device(): cols = lax.all_to_all(cols, 'dp', split_axis=1, concat_axis=0, tiled=True)  8.52 us
    transpose x1, other arithmetic, per_device(): hidden_all.transpose(0, 2, 1, 3, 4)  8.17 us
    all_to_all x1, waiting for transfers between devices, per_device(): lax.all_to_all(send_back, ('expert', 'dp'), split_axis=0, concat_axis=0,...  6.52 us
    transpose x1, local copies, waits for them, and re-layouts, per_device(): hidden_all.transpose(0, 2, 1, 3, 4)  4.53 us
    all_to_all x1, starting transfers between devices, per_device(): cols = lax.all_to_all(cols, 'dp', split_axis=1, concat_axis=0, tiled=True)  4.21 us
  transfers between devices with their start and end apart: 9, of which 6 were waited for; matrix products, arithmetic and copies ran while one was open for 12% of the time, Pallas kernels for 0%

profile of v5, /device:TPU:0, one launch (start us, length us, event | category | flops | bytes accessed | tf_op | source)
XLA Modules:
  0.0 172.2 jit_solution(12207095448207293238)
XLA Ops:
  7.2 1.5 copy.52
  8.6 0.2 copy.54
  8.9 0.8 convert_element_type.31
  9.6 0.7 pad_maximum_fusion.1
  10.3 0.1 copy.53
  10.5 0.1 broadcast_in_dim.112
  10.6 0.9 pad_maximum_fusion
  11.4 4.2 %all-to-all-start = ((bf16[132,4,512]{2,0,1:T(8,128)(2,1)}), bf16[132,4,512]{2,0,1:T(8,128)(2,1)S(1)}, u32[]{:S(2)}, u32[]{:S(2)}) async-start(bf16[132,4,512]{2,0,1:T(8,128)(2,1)} %pad_maximum_fusion), calls=%async_computation | async-start | bytes 1114112 | tf_op jit(solution)/shard_map/all_to_all | solution.py:83
  15.6 0.7 compare_and_fusion.1
  16.3 8.5 %all-to-all-done = bf16[132,4,512]{2,0,1:T(8,128)(2,1)S(1)} async-done(((bf16[132,4,512]{2,0,1:T(8,128)(2,1)}), bf16[132,4,512]{2,0,1:T(8,128)(2,1)S(1)}, u32[]{:S(2)}, u32[]{:S(2)}) %all-to-all-start) | async-done | bytes 540704 | tf_op jit(solution)/shard_map/all_to_all | solution.py:83
  24.8 0.6 gather_fusion
  25.4 0.9 broadcast_select_fusion
  26.3 1.8 %fusion.15 = (bf16[4,1,4,36,768]{4,2,3,1,0:T(4,128)(2,1)}, bf16[4,1,4,36,768]{4,2,3,1,0:T(4,128)(2,1)}) fusion(bf16[8,1,4,36,768]{4,2,3,1,0:T(4,128)(2,1)S(1)} %copy-done.2), kind=kLoop, calls=%fused_computation.47 | loop fusion | bytes 3538944 | tf_op jit(solution)/shard_map/slice | solution.py:89
  28.2 0.4 collective-permute-start
  28.5 1.7 collective-permute-start.1
  30.2 0.6 gather_fusion.1
  30.9 0.6 broadcast_in_dim.124
  31.5 0.5 collective-permute-start.3
  32.0 19.0 %collective-permute-done = bf16[4,1,4,36,768]{4,2,3,1,0:T(4,128)(2,1)S(1)} collective-permute-done((bf16[4,1,4,36,768]{4,2,3,1,0:T(4,128)(2,1)}, bf16[4,1,4,36,768]{4,2,3,1,0:T(4,128)(2,1)S(1)}, u32[]{:S(2)}, u32[]{:S(2)}) %collective-permute-start) | collective-permute-done | bytes 884768 | tf_op jit(solution)/shard_map/ppermute | solution.py:93
  51.0 17.4 %collective-permute-done.1 = bf16[4,1,4,36,768]{4,2,3,1,0:T(4,128)(2,1)S(1)} collective-permute-done((bf16[4,1,4,36,768]{4,2,3,1,0:T(4,128)(2,1)}, bf16[4,1,4,36,768]{4,2,3,1,0:T(4,128)(2,1)S(1)}, u32[]{:S(2)}, u32[]{:S(2)}) %collective-permute-start.1) | collective-permute-done | bytes 884768 | tf_op jit(solution)/shard_map/ppermute | solution.py:93
  68.4 0.6 fusion.9
  69.0 0.8 convolution_convert_fusion.3
  69.8 1.1 collective-permute-done.5
  70.9 8.2 %maximum_bitcast_fusion = bf16[8,4,4,36,768]{4,1,3,2,0:T(4,128)(2,1)} fusion(bf16[4,1,4,36,768]{4,2,3,1,0:T(4,128)(2,1)} %collective-permute-done.5, bf16[4,1,4,36,768]{4,2,3,1,0:T(4,128)(2,1)} %collective-permute-done.4, bf16[4,1,4,36,768]{4,2,3,1,0:T(4,128)(2,1)} %collective-permute-done.3, bf16[4,1,4,36,768]{4,2,3,1,0:T(4,128)(2,1)} %collective-permute-done.2, ...), kind=kLoop, calls=%fused_computation.3 | loop fusion | flops 21233664 | bytes 14155776 | tf_op jit(solution)/shard_map/transpose | solution.py:129
  79.1 4.5 %copy.55 = bf16[8,4,4,36,768]{4,3,2,1,0:T(8,128)(2,1)S(1)} copy(bf16[8,4,4,36,768]{4,1,3,2,0:T(4,128)(2,1)} %maximum_bitcast_fusion) | data formatting | bytes 14155776 | tf_op jit(solution)/shard_map/transpose | solution.py:129
  83.6 3.8 %pad.4.h_ref = bf16[8,16,40,768]{3,2,1,0:T(8,128)(2,1)} pad(bf16[8,16,36,768]{3,2,1,0:T(8,128)(2,1)S(1)} %bitcast.38, bf16[]{:T(256)} %constant.43.clone.1), padding=0_0x0_0x0_4x0_0 | pad | bytes 14942210 | tf_op jit(solution)/shard_map/jit(_pad)/pad | solution.py:130
  87.4 30.9 %all-gather.3.cloned.1.call-done = bf16[16,132,512]{2,1,0:T(8,128)(2,1)} async-done(((bf16[4,132,512]{2,1,0:T(8,128)(2,1)}), bf16[16,132,512]{2,1,0:T(8,128)(2,1)}) %all-gather.3.cloned.1.call-update) | async-done | bytes 2162704 | tf_op jit(solution)/shard_map/all_gather | solution.py:98
  118.3 1.1 slice.38
  119.3 0.4 reshape_reshape.3
  119.7 1.0 fusion.16
  120.7 1.2 copy.64
  121.9 0.2 copy.65
  122.1 0.1 compare_reduce_fusion
  122.3 0.1 fusion.8
  122.4 0.1 convolution_convert_fusion.2
  122.6 3.8 %convolution_convert_fusion.1.g_ref = bf16[16,8,40,512]{3,2,1,0:T(8,128)(2,1)} fusion(bf16[16,132,512]{2,1,0:T(8,128)(2,1)S(1)} %copy-done.1, s32[16,8,128]{2,1,0:T(8,128)S(1)} %convolution_convert_fusion.2, pred[16,8,128]{2,1,0:T(8,128)(4,1)S(1)} %bitcast.41), kind=kOutput, calls=%fused_computation.6 | convolution fusion | flops 675020800 | bytes 7421952 | tf_op jit(solution)/shard_map/blct,btd->blcd/dot_general | solution.py:121
  126.4 3.8 %convolution_convert_fusion.s_ref = bf16[16,8,40,512]{3,2,1,0:T(8,128)(2,1)} fusion(bf16[16,132,512]{2,1,0:T(8,128)(2,1)S(1)} %copy-done.1, bf16[16,8,128]{2,1,0:T(8,128)(2,1)S(1)} %bitcast.45, s32[16,8,128]{2,1,0:T(8,128)S(1)} %convolution_convert_fusion.2, pred[16,8,128]{2,1,0:T(8,128)(4,1)S(1)} %bitcast.42), kind=kOutput, calls=%fused_computation.5 | convolution fusion | flops 675676160 | bytes 7454720 | tf_op jit(solution)/shard_map/blct,btd->blcd/dot_general | solution.py:124
  130.2 18.1 %shard_map.86 = (f32[8,768,512]{2,1,0:T(8,128)}, f32[8,640,1]{2,1,0:T(8,128)}) custom-call(bf16[8,16,40,768]{3,2,1,0:T(8,128)(2,1)} %pad.4.h_ref, bf16[16,8,40,512]{3,2,1,0:T(8,128)(2,1)} %convolution_convert_fusion.s_ref, bf16[16,8,40,512]{3,2,1,0:T(8,128)(2,1)} %convolution_convert_fusion.1.g_ref, bf16[8,768,512]{2,1,0:T(8,128)(2,1)} %w_ref.1), custom_call_target="tpu_custom_call" | custom-call | tf_op jit(solution)/shard_map/pallas_call | solution.py:42
  148.3 2.5 %reduce = f32[8,640]{1,0:T(8,128)S(1)} reduce(f32[8,640,1]{2,1,0:T(8,128)} %get-tuple-element.9, f32[]{:T(128)} %constant.53), dimensions={2}, to_apply=%get-tuple-element.9.reduce_sub_computation | reduce | bytes 40964 | tf_op jit(solution)/shard_map/pallas_call | solution.py:42
  150.8 0.1 reshape.93
  150.9 0.6 gather_fusion.2
  151.6 0.7 reshape.126
  152.3 3.5 %all-to-all-start.1 = ((f32[16,1,288]{2,1,0:T(1,128)}), f32[16,1,288]{2,1,0:T(1,128)S(1)}, u32[]{:S(2)}, u32[]{:S(2)}) async-start(f32[16,1,288]{2,1,0:T(1,128)} %reshape.126), calls=%async_computation.1 | async-start | bytes 49152 | tf_op jit(solution)/shard_map/all_to_all | solution.py:137
  155.9 6.5 %all-to-all-done.1 = f32[16,1,288]{2,1,0:T(1,128)S(1)} async-done(((f32[16,1,288]{2,1,0:T(1,128)}), f32[16,1,288]{2,1,0:T(1,128)S(1)}, u32[]{:S(2)}, u32[]{:S(2)}) %all-to-all-start.1) | async-done | bytes 18464 | tf_op jit(solution)/shard_map/all_to_all | solution.py:137
  162.4 0.5 broadcast.102
  162.9 0.7 reduce.1
  163.8 0.8 select_reduce_fusion
  164.7 0.7 select_reduce_fusion.1
  (42 shorter events, 0.5 us)
Async XLA Ops:
  7.2 19.2 %copy-start.2 = (bf16[8,1,4,36,768]{4,2,3,1,0:T(4,128)(2,1)S(1)}, bf16[8,1,4,36,768]{4,2,3,1,0:T(4,128)(2,1)}, u32[]{:S(2)}) copy-start(bf16[8,1,4,36,768]{4,2,3,1,0:T(4,128)(2,1)} %param.10) | copy-start | bytes 5308420
  8.6 21.6 %copy-start = (s32[4]{0:T(128)S(1)}, s32[4]{0:T(128)}, u32[]{:S(2)}) copy-start(s32[4]{0:T(128)} %constant.49.clone) | copy-start | bytes 52
  8.9 59.5 %copy-start.4 = (s32[128,8]{0,1:T(8,128)S(1)}, s32[128,8]{0,1:T(8,128)}, u32[]{:S(2)}) copy-start(s32[128,8]{0,1:T(8,128)} %param.9) | copy-start | bytes 12292
  11.4 13.4 %all-to-all-start = ((bf16[132,4,512]{2,0,1:T(8,128)(2,1)}), bf16[132,4,512]{2,0,1:T(8,128)(2,1)S(1)}, u32[]{:S(2)}, u32[]{:S(2)}) async-start(bf16[132,4,512]{2,0,1:T(8,128)(2,1)} %pad_maximum_fusion), calls=%async_computation | async-start | bytes 1114112 | tf_op jit(solution)/shard_map/all_to_all | solution.py:83
  15.6 102.6 %all-gather.3.cloned.1.call-start = ((), (), s32[]{:S(2)}) async-start(), calls=%async_computation.2 | async-start | bytes 2785280 | tf_op jit(solution)/shard_map/all_gather | solution.py:98
  28.2 22.8 %collective-permute-start = (bf16[4,1,4,36,768]{4,2,3,1,0:T(4,128)(2,1)}, bf16[4,1,4,36,768]{4,2,3,1,0:T(4,128)(2,1)S(1)}, u32[]{:S(2)}, u32[]{:S(2)}) collective-permute-start(bf16[4,1,4,36,768]{4,2,3,1,0:T(4,128)(2,1)} %get-tuple-element.12), channel_id=1, source_target_pairs={{0,2},{1,3},{2,0},{3,1},{4,6},{5,7},{6,4},{7,5},{8,10},{9,11},{10,... | collective-permute-start | bytes 2654216 | tf_op jit(solution)/shard_map/ppermute | solution.py:93
  28.5 39.8 %collective-permute-start.1 = (bf16[4,1,4,36,768]{4,2,3,1,0:T(4,128)(2,1)}, bf16[4,1,4,36,768]{4,2,3,1,0:T(4,128)(2,1)S(1)}, u32[]{:S(2)}, u32[]{:S(2)}) collective-permute-start(bf16[4,1,4,36,768]{4,2,3,1,0:T(4,128)(2,1)} %get-tuple-element.13), channel_id=1, source_target_pairs={{0,2},{1,3},{2,0},{3,1},{4,6},{5,7},{6,4},{7,5},{8,10},{9,11},{10,... | collective-permute-start | bytes 2654216 | tf_op jit(solution)/shard_map/ppermute | solution.py:93
  31.5 38.3 %collective-permute-start.2 = (bf16[4,1,4,36,768]{4,2,3,1,0:T(4,128)(2,1)}, bf16[4,1,4,36,768]{4,2,3,1,0:T(4,128)(2,1)}, u32[]{:S(2)}, u32[]{:S(2)}) collective-permute-start(bf16[4,1,4,36,768]{4,2,3,1,0:T(4,128)(2,1)} %get-tuple-element.12), channel_id=1, source_target_pairs={{0,1},{1,0},{2,3},{3,2},{4,5},{5,4},{6,7},{7,6},{8,9},{9,8},{10,11... | collective-permute-start | bytes 2654216 | tf_op jit(solution)/shard_map/ppermute | solution.py:92
  31.5 38.3 %collective-permute-start.3 = (bf16[4,1,4,36,768]{4,2,3,1,0:T(4,128)(2,1)}, bf16[4,1,4,36,768]{4,2,3,1,0:T(4,128)(2,1)}, u32[]{:S(2)}, u32[]{:S(2)}) collective-permute-start(bf16[4,1,4,36,768]{4,2,3,1,0:T(4,128)(2,1)} %get-tuple-element.13), channel_id=1, source_target_pairs={{0,1},{1,0},{2,3},{3,2},{4,5},{5,4},{6,7},{7,6},{8,9},{9,8},{10,11... | collective-permute-start | bytes 2654216 | tf_op jit(solution)/shard_map/ppermute | solution.py:92
  51.0 18.9 %collective-permute-start.4 = (bf16[4,1,4,36,768]{4,2,3,1,0:T(4,128)(2,1)S(1)}, bf16[4,1,4,36,768]{4,2,3,1,0:T(4,128)(2,1)}, u32[]{:S(2)}, u32[]{:S(2)}) collective-permute-start(bf16[4,1,4,36,768]{4,2,3,1,0:T(4,128)(2,1)S(1)} %collective-permute-done), channel_id=1, source_target_pairs={{0,1},{1,0},{2,3},{3,2},{4,5},{5,4},{6,7},{7,6},{8,9},{9,8},{10,11... | collective-permute-start | bytes 2654216 | tf_op jit(solution)/shard_map/ppermute | solution.py:94
  68.3 2.6 %collective-permute-start.5 = (bf16[4,1,4,36,768]{4,2,3,1,0:T(4,128)(2,1)S(1)}, bf16[4,1,4,36,768]{4,2,3,1,0:T(4,128)(2,1)}, u32[]{:S(2)}, u32[]{:S(2)}) collective-permute-start(bf16[4,1,4,36,768]{4,2,3,1,0:T(4,128)(2,1)S(1)} %collective-permute-done.1), channel_id=1, source_target_pairs={{0,1},{1,0},{2,3},{3,2},{4,5},{5,4},{6,7},{7,6},{8,9},{9,8},{10,11... | collective-permute-start | bytes 2654216 | tf_op jit(solution)/shard_map/ppermute | solution.py:94
  118.3 4.3 %copy-start.1 = (bf16[16,132,512]{2,1,0:T(8,128)(2,1)S(1)}, bf16[16,132,512]{2,1,0:T(8,128)(2,1)}, u32[]{:S(2)}) copy-start(bf16[16,132,512]{2,1,0:T(8,128)(2,1)} %all-gather.3.cloned.1.call-done) | copy-start | bytes 6488068
  130.2 21.3 %copy-start.6 = (pred[16]{0:T(512)(128)(4,1)S(1)}, pred[16]{0:T(512)(128)(4,1)}, u32[]{:S(2)}) copy-start(pred[16]{0:T(512)(128)(4,1)} %broadcast_in_dim.124) | copy-start | bytes 52
  130.2 25.7 %copy-start.5 = (s32[128,32]{0,1:T(8,128)S(1)}, s32[128,32]{0,1:T(8,128)}, u32[]{:S(2)}) copy-start(s32[128,32]{0,1:T(8,128)} %convolution_convert_fusion.3) | copy-start | bytes 49156
  130.2 33.7 %copy-start.3 = (pred[128,8,32]{0,2,1:T(8,128)(4,1)S(1)}, pred[128,8,32]{0,2,1:T(8,128)(4,1)}, u32[]{:S(2)}) copy-start(pred[128,8,32]{0,2,1:T(8,128)(4,1)} %get-tuple-element.17) | copy-start | bytes 98308
  152.3 10.1 %all-to-all-start.1 = ((f32[16,1,288]{2,1,0:T(1,128)}), f32[16,1,288]{2,1,0:T(1,128)S(1)}, u32[]{:S(2)}, u32[]{:S(2)}) async-start(f32[16,1,288]{2,1,0:T(1,128)} %reshape.126), calls=%async_computation.1 | async-start | bytes 49152 | tf_op jit(solution)/shard_map/all_to_all | solution.py:137
Sparse Core Ops, SparseCore 0:
  68.5 49.7 all-gather.2
